TPU v7x, 512 devices: a whole 4x4x16 slice. The times are simulated.
512 devices in a mesh: dp: 8 (over y, core), tensor: 64 (over x, z).
Axes of the slice: x: 4, y: 4, z: 16, core: 2. Of those that a mesh axis runs over, the one named last changes fastest.
Arguments:
- hidden: bfloat16 [64, 256, 1536], P('dp', 'tensor'), may hold values from -24 to 24
- norm_gain: float32 [1536], replicated, may hold values from 0.1 to 1.9
- embedding: bfloat16 [49664, 1536], P('tensor'), may hold values from -2 to 2
- targets: int32 [64, 256], P('dp', 'tensor'), may hold values from 0 to 49154
- lengths: int32 [64], replicated, may hold values from 1 to 256, 10240 in all
- loss_mask: int32 [64, 256], P('dp', 'tensor'), may hold values 0 or 1
- deal_slots: int32 [64], replicated, may hold values from 0 to 63, as said below
Outputs:
- log_prob: float32 [64, 256], P('dp', 'tensor')
- entropy: float32 [64, 256], P('dp', 'tensor')
Inputs may be any that keep to these rules, and one draw needn't show every extreme that they name: A permutation; sequence k lies in data group deal_slots[k] // 8, and each data group's sequences go in equal numbers to every data group.
All inputs are finite; a program needn't handle non-finite values. No bound on the sum of `loss_mask` on one device may be relied on, other than what follows from the above.
Results may differ from a plain program's by a relative error of at most 0.012.
The roundings to bfloat16 on the way count: a program that leaves them out, or rounds other values in their place, can miss the bound.
Values may be sent and summed in bfloat16 or wider, within the bound.
No kernel may reach another device: no remote copies, remote signals or barrier semaphores. Data moves between devices by JAX's collectives and lax.ppermute only.
A program may use at most 64 MiB of HBM per device.

v0:
```python
import jax
import jax.numpy as jnp
from jax import lax
from jax.sharding import PartitionSpec as P

VREAL = 49155


def normalize(hidden, norm_gain):
    values = hidden.astype(jnp.float32)
    inverse = lax.rsqrt(jnp.mean(values * values, axis=2, keepdims=True) + 1e-05)
    return (values * inverse * norm_gain).astype(jnp.bfloat16)


def score(normed, marked, embedding):
    sequences, row_width = marked.shape
    vocab_rows = embedding.shape[0]
    tensor_rank = lax.axis_index("tensor")
    columns = tensor_rank * vocab_rows + jnp.arange(vocab_rows, dtype=jnp.int32)
    usable = columns < VREAL
    row_block = lax.all_gather(normed, "tensor", axis=1, tiled=True)
    block_marks = lax.all_gather(marked, "tensor", axis=1, tiled=True)
    row_count = row_block.shape[1]
    flat_rows = row_block.reshape(sequences * row_count, row_block.shape[2])
    logits = jnp.einsum("nd,vd->nv", flat_rows, embedding, preferred_element_type=jnp.float32)
    maximum = jnp.max(jnp.where(usable, logits, -jnp.inf), axis=1)
    weights = jnp.where(usable, jnp.exp(logits - maximum[:, None]), 0.0)
    totals = jnp.sum(weights, axis=1)
    weighted = jnp.sum(weights * jnp.where(usable, logits, 0.0), axis=1)
    chosen = jnp.sum(
        jnp.where(columns[None, :] == block_marks.reshape(-1)[:, None], logits, 0.0), axis=1
    )
    fresh_stats = (maximum, totals, weighted, chosen)
    maximum, totals, weighted, chosen = tuple(
        (updated.reshape(sequences, row_count) for updated in fresh_stats)
    )
    own_start = tensor_rank * row_width
    overall = lax.pmax(maximum, "tensor")
    factor = jnp.exp(maximum - overall)
    summed = lax.psum((totals * factor, weighted * factor, chosen), "tensor")
    totals, weighted, chosen = [
        lax.dynamic_slice_in_dim(member, own_start, row_width, 1) for member in summed
    ]
    maximum = lax.dynamic_slice_in_dim(overall, own_start, row_width, 1)
    log_total = maximum + jnp.log(totals)
    usable_rows = marked >= 0
    return (
        jnp.where(usable_rows, chosen - log_total, 0.0),
        jnp.where(usable_rows, log_total - weighted / totals, 0.0),
    )


def local(hidden, norm_gain, embedding, targets, lengths, loss_mask, deal_slots):
    group_rank = lax.axis_index("dp")
    sequences = hidden.shape[0]
    row_width = hidden.shape[1]
    tensor_rank = lax.axis_index("tensor")
    owned_seqs = group_rank * sequences + jnp.arange(sequences, dtype=jnp.int32)
    destination = deal_slots[owned_seqs] // sequences
    send_order = jnp.argsort(destination, stable=True)
    every_group = deal_slots // sequences
    arrived = jnp.argsort((every_group != group_rank).astype(jnp.int32), stable=True)[:sequences]
    arrived_slot = deal_slots[arrived] % sequences
    positions = tensor_rank * row_width + jnp.arange(row_width, dtype=jnp.int32)
    scored = (positions[None, :] < lengths[owned_seqs][:, None]) & (loss_mask == 1)
    marked = jnp.where(scored, targets, -1)
    normed = normalize(hidden, norm_gain)
    undo_order = jnp.argsort(send_order)
    came = lax.all_to_all(marked[send_order], "dp", split_axis=0, concat_axis=0, tiled=True)
    worker_marks = came[jnp.argsort(arrived_slot)]
    log_prob, entropy = score(normed, worker_marks, embedding)
    returned = (
        lax.all_to_all(log_prob[arrived_slot], "dp", split_axis=0, concat_axis=0, tiled=True),
        lax.all_to_all(entropy[arrived_slot], "dp", split_axis=0, concat_axis=0, tiled=True),
    )
    return (returned[0][undo_order], returned[1][undo_order])


def solution(mesh):
    placed = (
        P("dp", "tensor", None),
        P(),
        P("tensor", None),
        P("dp", "tensor"),
        P(),
        P("dp", "tensor"),
        P(),
    )
    return jax.shard_map(
        local,
        mesh=mesh,
        in_specs=placed,
        out_specs=(P("dp", "tensor"), P("dp", "tensor")),
        check_vma=False,
    )
```

profile of v0, /device:TPU:1, one launch (start us, length us, event | category | flops | bytes accessed | tf_op | source)
XLA Modules:
  0.0 627.9 jit_solution(17438690917976948653)
XLA Ops:
  7.2 1.2 fusion.1
  8.4 1.6 fusion.3
  11.6 1.3 gather_fusion
  12.9 1.3 gather_fusion.1
  14.9 2.0 sort.66
  17.9 1.1 gather_fusion.2
  19.1 10.1 %all-to-all-start = ((s32[8,1,4]{2,1,0:T(1,128)}), s32[8,1,4]{2,1,0:T(1,128)S(1)}, u32[]{:S(2)}, u32[]{:S(2)}) async-start(s32[8,1,4]{2,1,0:T(1,128)} %bitcast.14), calls=%async_computation | async-start | bytes 8192 | tf_op jit(solution)/shard_map/all_to_all | solution.py:69
  29.2 1.3 gather_fusion.3
  30.5 1.0 sort.68
  31.4 1.0 sort.67
  32.5 1.3 all-to-all-done
  34.4 79.1 %all-gather.1 = s32[64,4,8]{2,1,0:T(4,128)S(1)} all-gather(s32[1,4,8]{2,1,0:T(4,128)S(1)} %bitcast.35), channel_id=2, replica_groups=mesh['dp'=8,'tensor'=64] {'tensor'}, dimensions={0}, use_global_device_ids=true | all-gather | bytes 8320 | tf_op jit(solution)/shard_map/all_gather | solution.py:22
  113.6 45.4 %all-gather.4.cloned.1.call-done = bf16[8,256,1536]{2,0,1:T(8,128)(2,1)} async-done(((bf16[8,4,1536]{2,0,1:T(8,128)(2,1)}), bf16[8,256,1536]{2,0,1:T(8,128)(2,1)}) %all-gather.4.cloned.1.call-update) | async-done | bytes 6291472 | tf_op jit(solution)/shard_map/all_gather | solution.py:21
  159.0 4.8 copy.60
  163.9 7.0 %select_reduce_fusion = (f32[2048]{0:T(1024)S(1)}, f32[2048,776]{0,1:T(8,128)}) fusion(pred[776]{0:T(1024)(128)(4,1)S(1)} %broadcast_compare_fusion, bf16[2048,1536]{1,0:T(8,128)(2,1)S(1)} %bitcast.27, bf16[776,1536]{1,0:T(8,128)(2,1)S(1)} %copy-done), kind=kOutput, calls=%fused_computation.12 | convolution fusion | flops 4885346304 | bytes 15041288 | tf_op jit(solution)/shard_map/nd,vd->nv/dot_general | solution.py:25
  170.9 4.9 multiply_reduce_fusion
  175.8 114.4 %pmax.7 = f32[8,256]{1,0:T(8,128)S(1)} all-reduce(f32[8,256]{1,0:T(8,128)S(1)} %reshape.109), channel_id=1, replica_groups=mesh['dp'=8,'tensor'=64] {'tensor'}, use_global_device_ids=true, to_apply=%region_7.8 | all-reduce | flops 2048 | bytes 16384 | tf_op jit(solution)/shard_map/pmax | solution.py:38
  290.2 220.0 %all-reduce = (f32[8,256]{1,0:T(8,128)S(1)}, f32[8,256]{1,0:T(8,128)S(1)}, f32[8,256]{1,0:T(8,128)S(1)}) all-reduce(f32[8,256]{1,0:T(8,128)S(1)} %reshape.108, f32[8,256]{1,0:T(8,128)S(1)} %get-tuple-element.27, f32[8,256]{1,0:T(8,128)S(1)} %get-tuple-element.26), channel_id=1, replica_groups=mesh['dp'=8,'tensor'=64] {'tensor'}, use_global_device_ids=true, to_apply=%region_5.6 | all-reduce | flops 6144 | bytes 49152 | tf_op jit(solution)/shard_map/psum | solution.py:40
  510.4 1.1 gather_fusion.5
  511.6 95.2 %all-to-all-start.1 = ((f32[8,1,4]{2,1,0:T(1,128)}), f32[8,1,4]{2,1,0:T(1,128)S(1)}, u32[]{:S(2)}, u32[]{:S(2)}) async-start(f32[8,1,4]{2,1,0:T(1,128)} %bitcast.15), calls=%async_computation.1 | async-start | bytes 8192 | tf_op jit(solution)/shard_map/all_to_all | solution.py:73
  606.8 1.1 gather_fusion.7
  608.0 3.5 all-to-all-done.1
  611.4 3.8 all-to-all-start.2
  616.5 3.4 all-to-all-done.2
  (45 shorter events, 6.7 us)
Async XLA Ops:
  7.2 156.7 %copy-start = (bf16[776,1536]{1,0:T(8,128)(2,1)S(1)}, bf16[776,1536]{1,0:T(8,128)(2,1)}, u32[]{:S(2)}) copy-start(bf16[776,1536]{1,0:T(8,128)(2,1)} %param.9) | copy-start | bytes 7151620
  7.2 151.9 %all-gather.4.cloned.1.call-start = ((), (), s32[]{:S(2)}) async-start(), calls=%async_computation.3 | async-start | bytes 6389760 | tf_op jit(solution)/shard_map/all_gather | solution.py:21
  19.1 14.7 %all-to-all-start = ((s32[8,1,4]{2,1,0:T(1,128)}), s32[8,1,4]{2,1,0:T(1,128)S(1)}, u32[]{:S(2)}, u32[]{:S(2)}) async-start(s32[8,1,4]{2,1,0:T(1,128)} %bitcast.14), calls=%async_computation | async-start | bytes 8192 | tf_op jit(solution)/shard_map/all_to_all | solution.py:69
  511.6 99.8 %all-to-all-start.1 = ((f32[8,1,4]{2,1,0:T(1,128)}), f32[8,1,4]{2,1,0:T(1,128)S(1)}, u32[]{:S(2)}, u32[]{:S(2)}) async-start(f32[8,1,4]{2,1,0:T(1,128)} %bitcast.15), calls=%async_computation.1 | async-start | bytes 8192 | tf_op jit(solution)/shard_map/all_to_all | solution.py:73
  611.4 8.5 %all-to-all-start.2 = ((f32[8,1,4]{2,1,0:T(1,128)}), f32[8,1,4]{2,1,0:T(1,128)S(1)}, u32[]{:S(2)}, u32[]{:S(2)}) async-start(f32[8,1,4]{2,1,0:T(1,128)} %bitcast.16), calls=%async_computation.2 | async-start | bytes 8192 | tf_op jit(solution)/shard_map/all_to_all | solution.py:74
Sparse Core Ops, SparseCore 0:
  10.9 148.0 all-gather.3
where the time goes:
time: 628 us
  blocking collectives  414 us (66%)
  starting transfers between devices  109 us (17%)
  waiting for transfers between devices  53.6 us (9%)
  local copies, waits for them, and re-layouts  16.8 us (3%)
  between operations  14.2 us (2%)
  other arithmetic  13.6 us (2%)
  matrix products  7.04 us (1%)
    psum x1, blocking collectives, score(): summed = lax.psum((totals * factor, weighted * factor, chosen), 'tensor')  220 us
    pmax x1, blocking collectives, score(): overall = lax.pmax(maximum, 'tensor')  114 us
    all_to_all x1, starting transfers between devices, local(): lax.all_to_all(log_prob[arrived_slot], 'dp', split_axis=0, concat_axis=0,...  95.2 us
    all_gather x1, blocking collectives, score(): block_marks = lax.all_gather(marked, 'tensor', axis=1, tiled=True)  79.1 us
    all_gather x1, waiting for transfers between devices, score(): row_block = lax.all_gather(normed, 'tensor', axis=1, tiled=True)  45.4 us
  transfers between devices with their start and end apart: 4, of which 4 were waited for; matrix products, arithmetic and copies ran while one was open for 2% of the time, Pallas kernels for 0%

commit v1 on v0

v1 whole, which is shorter than its diff:
```python
import numpy as np
import jax
import jax.numpy as jnp
from jax import lax
from jax.sharding import Mesh
from jax.sharding import PartitionSpec as P

VREAL = 49155


def normalize(hidden, norm_gain):
    values = hidden.astype(jnp.float32)
    inverse = lax.rsqrt(jnp.mean(values * values, axis=2, keepdims=True) + 1e-05)
    return (values * inverse * norm_gain).astype(jnp.bfloat16)


def split_tensor(mesh):
    row = mesh.devices[0]
    slow = len({tuple(d.coords)[0] for d in row})
    if row.size % slow or slow in (1, row.size):
        return None
    return slow, row.size // slow


def local_fn(tensor_axes, tensor_size):
    def tensor_rank():
        if len(tensor_axes) == 1:
            return lax.axis_index(tensor_axes[0])
        return lax.axis_index(tensor_axes[0]) * tensor_size[1] + lax.axis_index(tensor_axes[1])

    def gather_rows(normed):
        rows = normed
        for name in tensor_axes:
            rows = lax.all_gather(rows, name, axis=1, tiled=True)
        return rows

    def to_gather_order(by_rank):
        s, w = by_rank.shape[1], by_rank.shape[2]
        if len(tensor_axes) == 1:
            return jnp.transpose(by_rank, (1, 0, 2)).reshape(-1)
        grid = by_rank.reshape(tensor_size[0], tensor_size[1], s, w)
        return jnp.transpose(grid, (2, 1, 0, 3)).reshape(-1)

    def from_gather_order(stats, s, w):
        k = stats.shape[0]
        if len(tensor_axes) == 1:
            return jnp.transpose(stats.reshape(k, s, tensor_size[0], w), (2, 0, 1, 3))
        grid = stats.reshape(k, s, tensor_size[1], tensor_size[0], w)
        grid = jnp.transpose(grid, (3, 2, 0, 1, 4))
        return grid.reshape(tensor_size[0] * tensor_size[1], k, s, w)

    def local(hidden, norm_gain, embedding, targets, lengths, loss_mask, deal_slots):
        group_rank = lax.axis_index("dp")
        sequences, row_width = hidden.shape[0], hidden.shape[1]
        ranks = int(np.prod(tensor_size))
        t_rank = tensor_rank()
        owned_seqs = group_rank * sequences + jnp.arange(sequences, dtype=jnp.int32)
        destination = deal_slots[owned_seqs] // sequences
        send_order = jnp.argsort(destination, stable=True)
        every_group = deal_slots // sequences
        arrived = jnp.argsort((every_group != group_rank).astype(jnp.int32), stable=True)[:sequences]
        arrived_slot = deal_slots[arrived] % sequences
        positions = t_rank * row_width + jnp.arange(row_width, dtype=jnp.int32)
        scored = (positions[None, :] < lengths[owned_seqs][:, None]) & (loss_mask == 1)
        marked = jnp.where(scored, targets, -1)
        undo_order = jnp.argsort(send_order)

        normed = normalize(hidden, norm_gain)
        row_block = gather_rows(normed)

        came = lax.all_to_all(marked[send_order], "dp", split_axis=0, concat_axis=0, tiled=True)
        worker_marks = came[jnp.argsort(arrived_slot)]
        spread = jnp.broadcast_to(worker_marks[None], (ranks,) + worker_marks.shape)
        block_marks = lax.all_to_all(spread, tensor_axes, split_axis=0, concat_axis=0, tiled=True)
        block_marks = to_gather_order(block_marks)

        vocab_rows = embedding.shape[0]
        columns = t_rank * vocab_rows + jnp.arange(vocab_rows, dtype=jnp.int32)
        usable = columns < VREAL
        flat_rows = row_block.reshape(-1, row_block.shape[2])
        logits = jnp.einsum("nd,vd->nv", flat_rows, embedding, preferred_element_type=jnp.float32)
        maximum = jnp.max(jnp.where(usable, logits, -jnp.inf), axis=1)
        weights = jnp.where(usable, jnp.exp(logits - maximum[:, None]), 0.0)
        totals = jnp.sum(weights, axis=1)
        weighted = jnp.sum(weights * jnp.where(usable, logits, 0.0), axis=1)
        chosen = jnp.sum(jnp.where(columns[None, :] == block_marks[:, None], logits, 0.0), axis=1)

        stats = from_gather_order(jnp.stack([maximum, totals, weighted, chosen]), sequences, row_width)
        parts = lax.all_to_all(stats, tensor_axes, split_axis=0, concat_axis=0, tiled=True)
        part_max, part_tot, part_wt, part_ch = parts[:, 0], parts[:, 1], parts[:, 2], parts[:, 3]
        overall = jnp.max(part_max, axis=0)
        factor = jnp.exp(part_max - overall[None])
        totals = jnp.sum(part_tot * factor, axis=0)
        weighted = jnp.sum(part_wt * factor, axis=0)
        chosen = jnp.sum(part_ch, axis=0)
        log_total = overall + jnp.log(totals)
        usable_rows = worker_marks >= 0
        log_prob = jnp.where(usable_rows, chosen - log_total, 0.0)
        entropy = jnp.where(usable_rows, log_total - weighted / totals, 0.0)

        both = jnp.stack([log_prob, entropy], axis=1)[arrived_slot]
        returned = lax.all_to_all(both, "dp", split_axis=0, concat_axis=0, tiled=True)[undo_order]
        return returned[:, 0], returned[:, 1]

    return local


def solution(mesh):
    split = split_tensor(mesh)
    if split is None:
        run_mesh, tensor_axes, tensor_size = mesh, ("tensor",), (mesh.shape["tensor"],)
    else:
        dp = mesh.shape["dp"]
        run_mesh = Mesh(mesh.devices.reshape(dp, split[0], split[1]), ("dp", "tx", "tz"))
        tensor_axes, tensor_size = ("tx", "tz"), split
    tensor = tensor_axes if len(tensor_axes) > 1 else tensor_axes[0]
    placed = (
        P("dp", tensor, None),
        P(),
        P(tensor, None),
        P("dp", tensor),
        P(),
        P("dp", tensor),
        P(),
    )
    return jax.shard_map(
        local_fn(tensor_axes, tensor_size),
        mesh=run_mesh,
        in_specs=placed,
        out_specs=(P("dp", tensor), P("dp", tensor)),
        check_vma=False,
    )
```

time: 628 us -> 187 us (0.30)
  blocking collectives: 414 us -> 10.8 us
  starting transfers between devices: 109 us -> 46.1 us
  waiting for transfers between devices: 53.6 us -> 73.3 us
    psum x1 -> x0, blocking collectives: 220 us -> none  [score(): summed = lax.psum((totals * factor, weighted * factor, chosen), 'tensor')]
    pmax x1 -> x0, blocking collectives: 114 us -> none  [score(): overall = lax.pmax(maximum, 'tensor')]
    all_gather x1, blocking collectives: 79.1 us -> 10.8 us  [gather_rows(): rows = lax.all_gather(rows, name, axis=1, tiled=True)]
    all_to_all x2 -> x3, starting transfers between devices: 99.1 us -> 34.3 us  [the longest x1 14.3 us: local(): lax.all_to_all(spread, tensor_axes, split_axis=0, concat_axis=0, tiled=True)]
    all_to_all x2 -> x3, waiting for transfers between devices: 6.88 us -> 34.1 us  [the longest x1 16.2 us: local(): lax.all_to_all(spread, tensor_axes, split_axis=0, concat_axis=0, tiled=True)]
  transfers between devices with their start and end apart: 4 -> 5, of which waited for: 4 -> 4; matrix products, arithmetic and copies ran while one was open for 2% -> 8% of each run, Pallas kernels for 0% -> 0%
where the time goes in v1:
time: 187 us; the launch traced here: 186 us
  waiting for transfers between devices  73.3 us (39%)
  starting transfers between devices  46.1 us (25%)
  local copies, waits for them, and re-layouts  18 us (10%)
  between operations  14.3 us (8%)
  other arithmetic  13.9 us (7%)
  blocking collectives  10.8 us (6%)
  matrix products  9.86 us (5%)
    all_gather x1, waiting for transfers between devices, gather_rows(): rows = lax.all_gather(rows, name, axis=1, tiled=True)  39.2 us
    all_to_all x1, waiting for transfers between devices, local(): lax.all_to_all(spread, tensor_axes, split_axis=0, concat_axis=0, tiled=True)  16.2 us
    all_to_all x1, starting transfers between devices, local(): lax.all_to_all(spread, tensor_axes, split_axis=0, concat_axis=0, tiled=True)  14.3 us
    all_to_all x1, starting transfers between devices, local(): lax.all_to_all(stats, tensor_axes, split_axis=0, concat_axis=0, tiled=True)  13.5 us
    all_to_all x1, waiting for transfers between devices, local(): lax.all_to_all(stats, tensor_axes, split_axis=0, concat_axis=0, tiled=True)  13.3 us
    all_to_all x1, starting transfers between devices, local(): lax.all_to_all(marked[send_order], 'dp', split_axis=0, concat_axis=0, til...  11.8 us
    all_gather x1, blocking collectives, gather_rows(): rows = lax.all_gather(rows, name, axis=1, tiled=True)  10.8 us
    dot_general x1, matrix products, local(): jnp.einsum('nd,vd->nv', flat_rows, embedding, preferred_element_type=jnp....  9.86 us
  transfers between devices with their start and end apart: 5, of which 4 were waited for; matrix products, arithmetic and copies ran while one was open for 8% of the time, Pallas kernels for 0%

profile of v1, /device:TPU:1, one launch (start us, length us, event | category | flops | bytes accessed | tf_op | source)
XLA Modules:
  0.0 186.3 jit_solution(15919900682084685579)
XLA Ops:
  7.2 1.2 fusion.1
  8.4 1.0 fusion.3
  9.4 10.8 %all_gather.6 = bf16[8,16,1536]{2,0,1:T(8,128)(2,1)S(1)} all-gather(bf16[8,4,1536]{2,0,1:T(8,128)(2,1)S(1)} %fusion.3), channel_id=1, replica_groups=mesh['dp'=8,'tx'=4,'tz'=16] {'tx'}, dimensions={1}, use_global_device_ids=true | all-gather | bytes 491520 | tf_op jit(solution)/shard_map/all_gather | solution.py:34
  20.2 0.9 copy.83
  22.6 1.3 gather_fusion
  23.9 1.3 gather_fusion.1
  25.2 1.0 sort.65
  26.3 1.1 gather_fusion.2
  27.4 11.8 %all-to-all-start = ((s32[8,1,4]{2,1,0:T(1,128)}), s32[8,1,4]{2,1,0:T(1,128)S(1)}, u32[]{:S(2)}, u32[]{:S(2)}) async-start(s32[8,1,4]{2,1,0:T(1,128)} %bitcast.18), calls=%async_computation | async-start | bytes 8192 | tf_op jit(solution)/shard_map/all_to_all | solution.py:71
  39.9 2.0 %sort.66 = (s32[64]{0:T(128)}, s32[64]{0:T(128)S(1)}) sort(s32[64]{0:T(128)S(1)} %compare_convert_fusion, s32[64]{0:T(128)S(1)} %iota.32), dimensions={0}, to_apply=%region_1.2 | sort | flops 384 | bytes 1024 | tf_op jit(solution)/shard_map/jit(argsort)/sort | solution.py:61
  41.9 1.3 gather_fusion.3
  43.2 1.0 sort.67
  45.6 14.3 %all-to-all-start.1 = ((s32[64,8,4]{1,2,0:T(4,128)}), s32[64,8,4]{1,2,0:T(4,128)S(1)}, u32[]{:S(2)}, u32[]{:S(2)}) async-start(s32[64,8,4]{1,2,0:T(4,128)} %broadcast_in_dim.60), calls=%async_computation.1 | async-start | bytes 262144 | tf_op jit(solution)/shard_map/all_to_all | solution.py:74
  59.9 1.0 sort.68
  60.9 16.2 %all-to-all-done.1 = s32[64,8,4]{1,2,0:T(4,128)S(1)} async-done(((s32[64,8,4]{1,2,0:T(4,128)}), s32[64,8,4]{1,2,0:T(4,128)S(1)}, u32[]{:S(2)}, u32[]{:S(2)}) %all-to-all-start.1) | async-done | bytes 8224 | tf_op jit(solution)/shard_map/all_to_all | solution.py:74
  77.8 39.2 %all-gather.2.cloned.1.call-done = bf16[8,256,1536]{2,1,0:T(8,128)(2,1)} async-done(((bf16[8,16,1536]{2,1,0:T(8,128)(2,1)}), bf16[8,256,1536]{2,1,0:T(8,128)(2,1)}) %all-gather.2.cloned.1.call-update) | async-done | bytes 6291472 | tf_op jit(solution)/shard_map/all_gather | solution.py:34
  117.0 9.9 %select_reduce_fusion.1 = (f32[2048]{0:T(1024)S(1)}, f32[2048,776]{0,1:T(8,128)}) fusion(pred[776]{0:T(1024)(128)(4,1)S(1)} %broadcast_compare_fusion, bf16[2048,1536]{1,0:T(8,128)(2,1)} %bitcast.65, bf16[776,1536]{1,0:T(8,128)(2,1)S(1)} %copy-done), kind=kOutput, calls=%fused_computation.11 | convolution fusion | flops 4885346304 | bytes 15041288 | tf_op jit(solution)/shard_map/nd,vd->nv/dot_general | solution.py:81
  127.2 4.9 %fusion = (f32[2048]{0:T(1024)S(1)}, f32[2048]{0:T(1024)S(1)}, f32[2048]{0:T(1024)S(1)}) fusion(f32[2048,776]{0,1:T(8,128)} %get-tuple-element.20, f32[2048]{0:T(1024)S(1)} %get-tuple-element.19, pred[776]{0:T(1024)(128)(4,1)S(1)} %broadcast_compare_fusion, s32[2048]{0:T(1024)S(1)} %eq.26, s32[776]{0:T(1024)S(1)} %iota_add_fusion), kind=kLoop, calls=%fused_computation.10 | loop fusion | flops 14297088 | bytes 6401832 | tf_op jit(solution)/shard_map/reduce_sum | solution.py:84
  134.8 1.1 reshape.238
  135.9 13.5 %all-to-all-start.2 = ((f32[64,1,128]{2,1,0:T(1,128)}), f32[64,1,128]{2,1,0:T(1,128)S(1)}, u32[]{:S(2)}, u32[]{:S(2)}) async-start(f32[64,1,128]{2,1,0:T(1,128)} %reshape.238), calls=%async_computation.2 | async-start | bytes 65536 | tf_op jit(solution)/shard_map/all_to_all | solution.py:89
  149.4 13.3 %all-to-all-done.2 = f32[64,1,128]{2,1,0:T(1,128)S(1)} async-done(((f32[64,1,128]{2,1,0:T(1,128)}), f32[64,1,128]{2,1,0:T(1,128)S(1)}, u32[]{:S(2)}, u32[]{:S(2)}) %all-to-all-start.2) | async-done | bytes 32800 | tf_op jit(solution)/shard_map/all_to_all | solution.py:89
  165.2 1.2 gather_fusion.5
  166.4 6.5 %all-to-all-start.3 = ((f32[8,2,4]{2,1,0:T(2,128)}), f32[8,2,4]{2,1,0:T(2,128)S(1)}, u32[]{:S(2)}, u32[]{:S(2)}) async-start(f32[8,2,4]{2,1,0:T(2,128)} %gather_fusion.5), calls=%async_computation.3 | async-start | bytes 16384 | tf_op jit(solution)/shard_map/all_to_all | solution.py:102
  172.9 4.6 %all-to-all-done.3 = f32[8,2,4]{2,1,0:T(2,128)S(1)} async-done(((f32[8,2,4]{2,1,0:T(2,128)}), f32[8,2,4]{2,1,0:T(2,128)S(1)}, u32[]{:S(2)}, u32[]{:S(2)}) %all-to-all-start.3) | async-done | bytes 288 | tf_op jit(solution)/shard_map/all_to_all | solution.py:102
  (63 shorter events, 11.8 us)
Async XLA Ops:
  7.2 109.8 %copy-start = (bf16[776,1536]{1,0:T(8,128)(2,1)S(1)}, bf16[776,1536]{1,0:T(8,128)(2,1)}, u32[]{:S(2)}) copy-start(bf16[776,1536]{1,0:T(8,128)(2,1)} %param.9) | copy-start | bytes 7151620
  7.2 109.8 %all-gather.2.cloned.1.call-start = ((), (), s32[]{:S(2)}) async-start(), calls=%async_computation.4 | async-start | bytes 6684672 | tf_op jit(solution)/shard_map/all_gather | solution.py:34
  27.4 16.8 %all-to-all-start = ((s32[8,1,4]{2,1,0:T(1,128)}), s32[8,1,4]{2,1,0:T(1,128)S(1)}, u32[]{:S(2)}, u32[]{:S(2)}) async-start(s32[8,1,4]{2,1,0:T(1,128)} %bitcast.18), calls=%async_computation | async-start | bytes 8192 | tf_op jit(solution)/shard_map/all_to_all | solution.py:71
  45.6 31.4 %all-to-all-start.1 = ((s32[64,8,4]{1,2,0:T(4,128)}), s32[64,8,4]{1,2,0:T(4,128)S(1)}, u32[]{:S(2)}, u32[]{:S(2)}) async-start(s32[64,8,4]{1,2,0:T(4,128)} %broadcast_in_dim.60), calls=%async_computation.1 | async-start | bytes 262144 | tf_op jit(solution)/shard_map/all_to_all | solution.py:74
  135.9 26.8 %all-to-all-start.2 = ((f32[64,1,128]{2,1,0:T(1,128)}), f32[64,1,128]{2,1,0:T(1,128)S(1)}, u32[]{:S(2)}, u32[]{:S(2)}) async-start(f32[64,1,128]{2,1,0:T(1,128)} %reshape.238), calls=%async_computation.2 | async-start | bytes 65536 | tf_op jit(solution)/shard_map/all_to_all | solution.py:89
  166.4 11.1 %all-to-all-start.3 = ((f32[8,2,4]{2,1,0:T(2,128)}), f32[8,2,4]{2,1,0:T(2,128)S(1)}, u32[]{:S(2)}, u32[]{:S(2)}) async-start(f32[8,2,4]{2,1,0:T(2,128)} %gather_fusion.5), calls=%async_computation.3 | async-start | bytes 16384 | tf_op jit(solution)/shard_map/all_to_all | solution.py:102
Sparse Core Ops, SparseCore 0:
  21.2 95.7 all-gather.1

commit v2 on v1

--- a/solution.py
+++ b/solution.py
@@ -2,10 +2,50 @@
 import jax
 import jax.numpy as jnp
 from jax import lax
+from jax.experimental import pallas as pl
+from jax.experimental.pallas import tpu as pltpu
 from jax.sharding import Mesh
 from jax.sharding import PartitionSpec as P
 
 VREAL = 49155
+INTERPRET = False
+ROW_BLOCK = 256
+
+
+def stats_kernel(offset_ref, rows_ref, emb_ref, marks_ref, out_ref):
+    logits = lax.dot_general(
+        rows_ref[...], emb_ref[...], (((1,), (1,)), ((), ())), preferred_element_type=jnp.float32
+    )
+    columns = offset_ref[0] + lax.broadcasted_iota(jnp.int32, logits.shape, 1)
+    usable = columns < VREAL
+    maximum = jnp.max(jnp.where(usable, logits, -jnp.inf), axis=1, keepdims=True)
+    weights = jnp.where(usable, jnp.exp(logits - maximum), 0.0)
+    totals = jnp.sum(weights, axis=1, keepdims=True)
+    weighted = jnp.sum(weights * jnp.where(usable, logits, 0.0), axis=1, keepdims=True)
+    chosen = jnp.sum(jnp.where(columns == marks_ref[...], logits, 0.0), axis=1, keepdims=True)
+    out_ref[...] = jnp.concatenate([maximum, totals, weighted, chosen], axis=1)
+
+
+def row_stats(rows, embedding, marks, offset):
+    n, d = rows.shape
+    v = embedding.shape[0]
+    block = ROW_BLOCK if n % ROW_BLOCK == 0 else n
+    return pl.pallas_call(
+        stats_kernel,
+        grid=(n // block,),
+        in_specs=[
+            pl.BlockSpec(memory_space=pltpu.SMEM),
+            pl.BlockSpec((block, d), lambda i: (i, 0)),
+            pl.BlockSpec((v, d), lambda i: (0, 0)),
+            pl.BlockSpec((block, 1), lambda i: (i, 0)),
+        ],
+        out_specs=pl.BlockSpec((block, 4), lambda i: (i, 0)),
+        out_shape=jax.ShapeDtypeStruct((n, 4), jnp.float32),
+        cost_estimate=pl.CostEstimate(
+            flops=2 * n * v * d, transcendentals=n * v, bytes_accessed=2 * (n + v) * d + 20 * n
+        ),
+        interpret=INTERPRET,
+    )(offset.reshape(1), rows, embedding, marks.reshape(n, 1))
 
 
 def normalize(hidden, norm_gain):
@@ -74,18 +114,11 @@
         block_marks = lax.all_to_all(spread, tensor_axes, split_axis=0, concat_axis=0, tiled=True)
         block_marks = to_gather_order(block_marks)
 
-        vocab_rows = embedding.shape[0]
-        columns = t_rank * vocab_rows + jnp.arange(vocab_rows, dtype=jnp.int32)
-        usable = columns < VREAL
+        offset = (t_rank * embedding.shape[0]).astype(jnp.int32)
         flat_rows = row_block.reshape(-1, row_block.shape[2])
-        logits = jnp.einsum("nd,vd->nv", flat_rows, embedding, preferred_element_type=jnp.float32)
-        maximum = jnp.max(jnp.where(usable, logits, -jnp.inf), axis=1)
-        weights = jnp.where(usable, jnp.exp(logits - maximum[:, None]), 0.0)
-        totals = jnp.sum(weights, axis=1)
-        weighted = jnp.sum(weights * jnp.where(usable, logits, 0.0), axis=1)
-        chosen = jnp.sum(jnp.where(columns[None, :] == block_marks[:, None], logits, 0.0), axis=1)
+        local_stats = row_stats(flat_rows, embedding, block_marks, offset)
 
-        stats = from_gather_order(jnp.stack([maximum, totals, weighted, chosen]), sequences, row_width)
+        stats = from_gather_order(jnp.transpose(local_stats), sequences, row_width)
         parts = lax.all_to_all(stats, tensor_axes, split_axis=0, concat_axis=0, tiled=True)
         part_max, part_tot, part_wt, part_ch = parts[:, 0], parts[:, 1], parts[:, 2], parts[:, 3]
         overall = jnp.max(part_max, axis=0)

time: 187 us -> 193 us (1.032)
  Pallas kernels: 0 us -> 13.7 us
  matrix products: 9.86 us -> 0 us
  local copies, waits for them, and re-layouts: 18 us -> 25.1 us
  other arithmetic: 13.9 us -> 8.79 us
    pallas_call x0 -> x1, Pallas kernels: none -> 13.7 us  [row_stats(): pl.pallas_call(stats_kernel, grid=(n // block,), in_specs=[pl.BlockSpec(m...]
    dot_general x1 -> x0, matrix products: 9.86 us -> none  [local(): jnp.einsum('nd,vd->nv', flat_rows, embedding, preferred_element_type=jnp....]
    all_gather x1, local copies, waits for them, and re-layouts: 0.86 us -> 7.46 us  [gather_rows(): rows = lax.all_gather(rows, name, axis=1, tiled=True)]
    reduce_sum x1 -> x0, other arithmetic: 4.94 us -> none  [local(): totals = jnp.sum(weights, axis=1)]
    reshape x1, local copies, waits for them, and re-layouts: 0.36 us -> 2.85 us  [from_gather_order(): return grid.reshape(tensor_size[0] * tensor_size[1], k, s, w)]
where the time goes in v2:
time: 193 us; the launch traced here: 192 us
  waiting for transfers between devices  73.1 us (38%)
  starting transfers between devices  46 us (24%)
  local copies, waits for them, and re-layouts  25.1 us (13%)
  between operations  14.2 us (7%)
  Pallas kernels  13.7 us (7%)
  blocking collectives  11.5 us (6%)
  other arithmetic  8.79 us (5%)
    all_gather x1, waiting for transfers between devices, gather_rows(): rows = lax.all_gather(rows, name, axis=1, tiled=True)  39.1 us
    all_to_all x1, waiting for transfers between devices, local(): lax.all_to_all(spread, tensor_axes, split_axis=0, concat_axis=0, tiled=True)  16.1 us
    all_to_all x1, starting transfers between devices, local(): lax.all_to_all(spread, tensor_axes, split_axis=0, concat_axis=0, tiled=True)  14.4 us
    pallas_call x1, Pallas kernels, row_stats(): pl.pallas_call(stats_kernel, grid=(n // block,), in_specs=[pl.BlockSpec(m...  13.7 us
    all_to_all x1, waiting for transfers between devices, local(): lax.all_to_all(stats, tensor_axes, split_axis=0, concat_axis=0, tiled=True)  13.3 us
    all_to_all x1, starting transfers between devices, local(): lax.all_to_all(stats, tensor_axes, split_axis=0, concat_axis=0, tiled=True)  13.3 us
    all_to_all x1, starting transfers between devices, local(): lax.all_to_all(marked[send_order], 'dp', split_axis=0, concat_axis=0, til...  11.8 us
    all_gather x1, blocking collectives, gather_rows(): rows = lax.all_gather(rows, name, axis=1, tiled=True)  11.5 us
  transfers between devices with their start and end apart: 5, of which 4 were waited for; matrix products, arithmetic and copies ran while one was open for 8% of the time, Pallas kernels for 0%

profile of v2, /device:TPU:1, one launch (start us, length us, event | category | flops | bytes accessed | tf_op | source)
XLA Modules:
  0.0 192.4 jit_solution(16997867427896009736)
XLA Ops:
  7.2 1.0 fusion
  8.2 1.0 fusion.2
  9.2 11.5 %all_gather.6 = bf16[8,16,1536]{2,0,1:T(8,128)(2,1)} all-gather(bf16[8,4,1536]{2,0,1:T(8,128)(2,1)S(1)} %fusion.2), channel_id=1, replica_groups=mesh['dp'=8,'tx'=4,'tz'=16] {'tx'}, dimensions={1}, use_global_device_ids=true | all-gather | bytes 491520 | tf_op jit(solution)/shard_map/all_gather | solution.py:74
  23.0 1.3 gather_fusion.1
  24.3 1.0 sort.65
  25.4 1.1 gather_fusion.2
  26.5 11.8 %all-to-all-start = ((s32[8,1,4]{2,1,0:T(1,128)}), s32[8,1,4]{2,1,0:T(1,128)S(1)}, u32[]{:S(2)}, u32[]{:S(2)}) async-start(s32[8,1,4]{2,1,0:T(1,128)} %bitcast.21), calls=%async_computation | async-start | bytes 8192 | tf_op jit(solution)/shard_map/all_to_all | solution.py:111
  39.0 2.0 %sort.66 = (s32[64]{0:T(128)}, s32[64]{0:T(128)S(1)}) sort(s32[64]{0:T(128)S(1)} %compare_convert_fusion, s32[64]{0:T(128)S(1)} %iota.27), dimensions={0}, to_apply=%region_1.2 | sort | flops 384 | bytes 1024 | tf_op jit(solution)/shard_map/jit(argsort)/sort | solution.py:101
  41.0 1.3 gather_fusion.3
  42.3 1.0 sort.67
  44.6 14.4 %all-to-all-start.1 = ((s32[64,8,4]{1,2,0:T(4,128)}), s32[64,8,4]{1,2,0:T(4,128)S(1)}, u32[]{:S(2)}, u32[]{:S(2)}) async-start(s32[64,8,4]{1,2,0:T(4,128)} %broadcast_in_dim.39), calls=%async_computation.1 | async-start | bytes 262144 | tf_op jit(solution)/shard_map/all_to_all | solution.py:114
  59.0 1.0 sort.68
  60.0 16.1 %all-to-all-done.1 = s32[64,8,4]{1,2,0:T(4,128)S(1)} async-done(((s32[64,8,4]{1,2,0:T(4,128)}), s32[64,8,4]{1,2,0:T(4,128)S(1)}, u32[]{:S(2)}, u32[]{:S(2)}) %all-to-all-start.1) | async-done | bytes 8224 | tf_op jit(solution)/shard_map/all_to_all | solution.py:114
  76.6 1.4 reshape_reshape.4.marks_ref
  77.9 39.1 %all-gather.2.cloned.1.call-done = bf16[8,256,1536]{2,0,1:T(8,128)(2,1)} async-done(((bf16[8,16,1536]{2,0,1:T(8,128)(2,1)}), bf16[8,256,1536]{2,0,1:T(8,128)(2,1)}) %all-gather.2.cloned.1.call-update) | async-done | bytes 6291472 | tf_op jit(solution)/shard_map/all_gather | solution.py:74
  117.0 7.5 %copy.70 = bf16[8,256,1536]{2,1,0:T(8,128)(2,1)} copy(bf16[8,256,1536]{2,0,1:T(8,128)(2,1)} %all-gather.2.cloned.1.call-done) | data formatting | bytes 12582912 | tf_op jit(solution)/shard_map/all_gather | solution.py:74
  124.5 13.7 %shard_map.86 = f32[2048,4]{1,0:T(8,128)} custom-call(s32[1]{0:T(128)} %bitcast.3.offset_ref, bf16[2048,1536]{1,0:T(8,128)(2,1)} %bitcast.58, bf16[776,1536]{1,0:T(8,128)(2,1)} %emb_ref.1, s32[2048,1]{1,0:T(8,128)} %reshape_reshape.4.marks_ref), custom_call_target="tpu_custom_call" | custom-call | flops 4882169856 | bytes 8716288 | tf_op jit(solution)/shard_map/pallas_call | solution.py:33
  138.2 2.9 %copy.99 = f32[4,16,4,8,4]{3,4,2,1,0:T(4,128)S(1)} copy(f32[4,16,4,8,4]{2,4,0,1,3:T(4,128)} %bitcast.63) | data formatting | bytes 65536 | tf_op jit(solution)/shard_map/reshape | solution.py:90
  141.0 1.1 reshape.231
  142.2 13.3 %all-to-all-start.2 = ((f32[64,1,128]{2,1,0:T(1,128)}), f32[64,1,128]{2,1,0:T(1,128)S(1)}, u32[]{:S(2)}, u32[]{:S(2)}) async-start(f32[64,1,128]{2,1,0:T(1,128)} %reshape.231), calls=%async_computation.2 | async-start | bytes 65536 | tf_op jit(solution)/shard_map/all_to_all | solution.py:122
  155.5 13.3 %all-to-all-done.2 = f32[64,1,128]{2,1,0:T(1,128)S(1)} async-done(((f32[64,1,128]{2,1,0:T(1,128)}), f32[64,1,128]{2,1,0:T(1,128)S(1)}, u32[]{:S(2)}, u32[]{:S(2)}) %all-to-all-start.2) | async-done | bytes 32800 | tf_op jit(solution)/shard_map/all_to_all | solution.py:122
  171.3 1.2 gather_fusion.5
  172.5 6.5 %all-to-all-start.3 = ((f32[8,2,4]{2,1,0:T(2,128)}), f32[8,2,4]{2,1,0:T(2,128)S(1)}, u32[]{:S(2)}, u32[]{:S(2)}) async-start(f32[8,2,4]{2,1,0:T(2,128)} %gather_fusion.5), calls=%async_computation.3 | async-start | bytes 16384 | tf_op jit(solution)/shard_map/all_to_all | solution.py:135
  179.0 4.6 %all-to-all-done.3 = f32[8,2,4]{2,1,0:T(2,128)S(1)} async-done(((f32[8,2,4]{2,1,0:T(2,128)}), f32[8,2,4]{2,1,0:T(2,128)S(1)}, u32[]{:S(2)}, u32[]{:S(2)}) %all-to-all-start.3) | async-done | bytes 288 | tf_op jit(solution)/shard_map/all_to_all | solution.py:135
  (51 shorter events, 9.2 us)
Async XLA Ops:
  7.2 15.2 %copy-start = (s32[64]{0:T(128)S(1)}, s32[64]{0:T(128)}, u32[]{:S(2)}) copy-start(s32[64]{0:T(128)} %param.11) | copy-start | bytes 772
  7.2 109.8 %all-gather.2.cloned.1.call-start = ((), (), s32[]{:S(2)}) async-start(), calls=%async_computation.4 | async-start | bytes 6684672 | tf_op jit(solution)/shard_map/all_gather | solution.py:74
  26.5 16.8 %all-to-all-start = ((s32[8,1,4]{2,1,0:T(1,128)}), s32[8,1,4]{2,1,0:T(1,128)S(1)}, u32[]{:S(2)}, u32[]{:S(2)}) async-start(s32[8,1,4]{2,1,0:T(1,128)} %bitcast.21), calls=%async_computation | async-start | bytes 8192 | tf_op jit(solution)/shard_map/all_to_all | solution.py:111
  44.6 31.4 %all-to-all-start.1 = ((s32[64,8,4]{1,2,0:T(4,128)}), s32[64,8,4]{1,2,0:T(4,128)S(1)}, u32[]{:S(2)}, u32[]{:S(2)}) async-start(s32[64,8,4]{1,2,0:T(4,128)} %broadcast_in_dim.39), calls=%async_computation.1 | async-start | bytes 262144 | tf_op jit(solution)/shard_map/all_to_all | solution.py:114
  142.2 26.6 %all-to-all-start.2 = ((f32[64,1,128]{2,1,0:T(1,128)}), f32[64,1,128]{2,1,0:T(1,128)S(1)}, u32[]{:S(2)}, u32[]{:S(2)}) async-start(f32[64,1,128]{2,1,0:T(1,128)} %reshape.231), calls=%async_computation.2 | async-start | bytes 65536 | tf_op jit(solution)/shard_map/all_to_all | solution.py:122
  172.5 11.1 %all-to-all-start.3 = ((f32[8,2,4]{2,1,0:T(2,128)}), f32[8,2,4]{2,1,0:T(2,128)S(1)}, u32[]{:S(2)}, u32[]{:S(2)}) async-start(f32[8,2,4]{2,1,0:T(2,128)} %gather_fusion.5), calls=%async_computation.3 | async-start | bytes 16384 | tf_op jit(solution)/shard_map/all_to_all | solution.py:135
Sparse Core Ops, SparseCore 0:
  20.9 96.0 all-gather.1

commit v3 on v2

--- a/solution.py
+++ b/solution.py
@@ -13,9 +13,7 @@
 
 
 def stats_kernel(offset_ref, rows_ref, emb_ref, marks_ref, out_ref):
-    logits = lax.dot_general(
-        rows_ref[...], emb_ref[...], (((1,), (1,)), ((), ())), preferred_element_type=jnp.float32
-    )
+    logits = jnp.dot(rows_ref[...], emb_ref[...], preferred_element_type=jnp.float32)
     columns = offset_ref[0] + lax.broadcasted_iota(jnp.int32, logits.shape, 1)
     usable = columns < VREAL
     maximum = jnp.max(jnp.where(usable, logits, -jnp.inf), axis=1, keepdims=True)
@@ -26,9 +24,9 @@
     out_ref[...] = jnp.concatenate([maximum, totals, weighted, chosen], axis=1)
 
 
-def row_stats(rows, embedding, marks, offset):
+def row_stats(rows, emb_t, marks, offset):
     n, d = rows.shape
-    v = embedding.shape[0]
+    v = emb_t.shape[1]
     block = ROW_BLOCK if n % ROW_BLOCK == 0 else n
     return pl.pallas_call(
         stats_kernel,
@@ -36,7 +34,7 @@
         in_specs=[
             pl.BlockSpec(memory_space=pltpu.SMEM),
             pl.BlockSpec((block, d), lambda i: (i, 0)),
-            pl.BlockSpec((v, d), lambda i: (0, 0)),
+            pl.BlockSpec((d, v), lambda i: (0, 0)),
             pl.BlockSpec((block, 1), lambda i: (i, 0)),
         ],
         out_specs=pl.BlockSpec((block, 4), lambda i: (i, 0)),
@@ -45,7 +43,7 @@
             flops=2 * n * v * d, transcendentals=n * v, bytes_accessed=2 * (n + v) * d + 20 * n
         ),
         interpret=INTERPRET,
-    )(offset.reshape(1), rows, embedding, marks.reshape(n, 1))
+    )(offset.reshape(1), rows, emb_t, marks.reshape(n, 1))
 
 
 def normalize(hidden, norm_gain):
@@ -77,16 +75,16 @@
     def to_gather_order(by_rank):
         s, w = by_rank.shape[1], by_rank.shape[2]
         if len(tensor_axes) == 1:
-            return jnp.transpose(by_rank, (1, 0, 2)).reshape(-1)
+            return jnp.transpose(by_rank, (0, 2, 1)).reshape(-1)
         grid = by_rank.reshape(tensor_size[0], tensor_size[1], s, w)
-        return jnp.transpose(grid, (2, 1, 0, 3)).reshape(-1)
+        return jnp.transpose(grid, (1, 0, 3, 2)).reshape(-1)
 
     def from_gather_order(stats, s, w):
         k = stats.shape[0]
         if len(tensor_axes) == 1:
-            return jnp.transpose(stats.reshape(k, s, tensor_size[0], w), (2, 0, 1, 3))
-        grid = stats.reshape(k, s, tensor_size[1], tensor_size[0], w)
-        grid = jnp.transpose(grid, (3, 2, 0, 1, 4))
+            return jnp.transpose(stats.reshape(k, tensor_size[0], w, s), (1, 0, 3, 2))
+        grid = stats.reshape(k, tensor_size[1], tensor_size[0], w, s)
+        grid = jnp.transpose(grid, (2, 1, 0, 4, 3))
         return grid.reshape(tensor_size[0] * tensor_size[1], k, s, w)
 
     def local(hidden, norm_gain, embedding, targets, lengths, loss_mask, deal_slots):
@@ -115,8 +113,8 @@
         block_marks = to_gather_order(block_marks)
 
         offset = (t_rank * embedding.shape[0]).astype(jnp.int32)
-        flat_rows = row_block.reshape(-1, row_block.shape[2])
-        local_stats = row_stats(flat_rows, embedding, block_marks, offset)
+        flat_rows = jnp.transpose(row_block, (1, 0, 2)).reshape(-1, row_block.shape[2])
+        local_stats = row_stats(flat_rows, jnp.transpose(embedding), block_marks, offset)
 
         stats = from_gather_order(jnp.transpose(local_stats), sequences, row_width)
         parts = lax.all_to_all(stats, tensor_axes, split_axis=0, concat_axis=0, tiled=True)

time: 193 us -> 186 us (0.964)
  local copies, waits for them, and re-layouts: 25.1 us -> 19.9 us
  waiting for transfers between devices: 73.1 us -> 70.7 us
    all_gather x1 -> x0, local copies, waits for them, and re-layouts: 7.46 us -> none  [gather_rows(): rows = lax.all_gather(rows, name, axis=1, tiled=True)]
    reshape x1 -> x0, local copies, waits for them, and re-layouts: 2.85 us -> none  [from_gather_order(): return grid.reshape(tensor_size[0] * tensor_size[1], k, s, w)]
    unnamed x6 -> x9, local copies, waits for them, and re-layouts: 3.32 us -> 6.16 us
    all_to_all x1, waiting for transfers between devices: 16.1 us -> 13.3 us  [local(): lax.all_to_all(spread, tensor_axes, split_axis=0, concat_axis=0, tiled=True)]
    transpose x1 -> x2, local copies, waits for them, and re-layouts: 0.47 us -> 2.85 us  [the longest x1 2.83 us: from_gather_order(): grid = jnp.transpose(grid, (2, 1, 0, 4, 3))]
  transfers between devices with their start and end apart: 5 -> 5, of which waited for: 4 -> 4; matrix products, arithmetic and copies ran while one was open for 8% -> 9% of each run, Pallas kernels for 0% -> 0%
where the time goes in v3:
time: 186 us; the launch traced here: 185 us
  waiting for transfers between devices  70.7 us (38%)
  starting transfers between devices  46 us (25%)
  local copies, waits for them, and re-layouts  19.9 us (11%)
  between operations  14.2 us (8%)
  Pallas kernels  13.8 us (7%)
  blocking collectives  11.5 us (6%)
  other arithmetic  8.94 us (5%)
    all_gather x1, waiting for transfers between devices, gather_rows(): rows = lax.all_gather(rows, name, axis=1, tiled=True)  39.5 us
    all_to_all x1, starting transfers between devices, local(): lax.all_to_all(spread, tensor_axes, split_axis=0, concat_axis=0, tiled=True)  14.4 us
    pallas_call x1, Pallas kernels, row_stats(): pl.pallas_call(stats_kernel, grid=(n // block,), in_specs=[pl.BlockSpec(m...  13.8 us
    all_to_all x1, starting transfers between devices, local(): lax.all_to_all(stats, tensor_axes, split_axis=0, concat_axis=0, tiled=True)  13.3 us
    all_to_all x1, waiting for transfers between devices, local(): lax.all_to_all(stats, tensor_axes, split_axis=0, concat_axis=0, tiled=True)  13.3 us
    all_to_all x1, waiting for transfers between devices, local(): lax.all_to_all(spread, tensor_axes, split_axis=0, concat_axis=0, tiled=True)  13.3 us
    all_to_all x1, starting transfers between devices, local(): lax.all_to_all(marked[send_order], 'dp', split_axis=0, concat_axis=0, til...  11.7 us
    all_gather x1, blocking collectives, gather_rows(): rows = lax.all_gather(rows, name, axis=1, tiled=True)  11.5 us
  transfers between devices with their start and end apart: 5, of which 4 were waited for; matrix products, arithmetic and copies ran while one was open for 9% of the time, Pallas kernels for 0%

profile of v3, /device:TPU:1, one launch (start us, length us, event | category | flops | bytes accessed | tf_op | source)
XLA Modules:
  0.0 185.2 jit_solution(12865898749202620366)
XLA Ops:
  7.2 1.2 fusion
  8.4 1.0 fusion.2
  9.4 11.5 %all_gather.6 = bf16[8,16,1536]{2,0,1:T(8,128)(2,1)} all-gather(bf16[8,4,1536]{2,0,1:T(8,128)(2,1)S(1)} %fusion.2), channel_id=1, replica_groups=mesh['dp'=8,'tx'=4,'tz'=16] {'tx'}, dimensions={1}, use_global_device_ids=true | all-gather | bytes 491520 | tf_op jit(solution)/shard_map/all_gather | solution.py:72
  23.2 1.3 gather_fusion.1
  24.5 1.0 sort.65
  25.5 1.1 gather_fusion.2
  26.7 11.7 %all-to-all-start = ((s32[8,1,4]{2,1,0:T(1,128)}), s32[8,1,4]{2,1,0:T(1,128)S(1)}, u32[]{:S(2)}, u32[]{:S(2)}) async-start(s32[8,1,4]{2,1,0:T(1,128)} %bitcast.23), calls=%async_computation | async-start | bytes 8192 | tf_op jit(solution)/shard_map/all_to_all | solution.py:109
  39.1 2.0 %sort.66 = (s32[64]{0:T(128)}, s32[64]{0:T(128)S(1)}) sort(s32[64]{0:T(128)S(1)} %compare_convert_fusion, s32[64]{0:T(128)S(1)} %iota.27), dimensions={0}, to_apply=%region_1.2 | sort | flops 384 | bytes 1024 | tf_op jit(solution)/shard_map/jit(argsort)/sort | solution.py:99
  41.1 1.3 gather_fusion.3
  42.4 1.0 sort.67
  44.7 14.4 %all-to-all-start.1 = ((s32[64,8,4]{1,2,0:T(4,128)}), s32[64,8,4]{1,2,0:T(4,128)S(1)}, u32[]{:S(2)}, u32[]{:S(2)}) async-start(s32[64,8,4]{1,2,0:T(4,128)} %broadcast_in_dim.39), calls=%async_computation.1 | async-start | bytes 262144 | tf_op jit(solution)/shard_map/all_to_all | solution.py:112
  59.2 2.8 %copy.74 = bf16[776,1536]{0,1:T(8,128)(2,1)} copy(bf16[776,1536]{1,0:T(8,128)(2,1)S(1)} %copy-done.1) | data formatting | bytes 4767744 | tf_op args[2]
  62.0 1.0 sort.68
  63.0 13.3 %all-to-all-done.1 = s32[64,8,4]{1,2,0:T(4,128)S(1)} async-done(((s32[64,8,4]{1,2,0:T(4,128)}), s32[64,8,4]{1,2,0:T(4,128)S(1)}, u32[]{:S(2)}, u32[]{:S(2)}) %all-to-all-start.1) | async-done | bytes 8224 | tf_op jit(solution)/shard_map/all_to_all | solution.py:112
  76.3 1.3 reshape_reshape.4.marks_ref
  77.6 39.5 %all-gather.2.cloned.1.call-done = bf16[8,256,1536]{2,0,1:T(8,128)(2,1)} async-done(((bf16[8,16,1536]{2,0,1:T(8,128)(2,1)}), bf16[8,256,1536]{2,0,1:T(8,128)(2,1)}) %all-gather.2.cloned.1.call-update) | async-done | bytes 6291472 | tf_op jit(solution)/shard_map/all_gather | solution.py:72
  117.1 13.8 %shard_map.86 = f32[2048,4]{1,0:T(8,128)} custom-call(s32[1]{0:T(128)} %bitcast.3.offset_ref, bf16[2048,1536]{1,0:T(8,128)(2,1)} %bitcast.73, bf16[1536,776]{1,0:T(8,128)(2,1)} %bitcast.61, s32[2048,1]{1,0:T(8,128)} %reshape_reshape.4.marks_ref), custom_call_target="tpu_custom_call" | custom-call | flops 4882169856 | bytes 8716288 | tf_op jit(solution)/shard_map/pallas_call | solution.py:31
  130.9 2.8 %copy.108 = f32[4,16,4,4,8]{4,3,0,1,2:T(4,128)S(1)} copy(f32[4,16,4,4,8]{0,4,3,2,1:T(8,128)} %bitcast.66) | data formatting | bytes 65536 | tf_op jit(solution)/shard_map/transpose | solution.py:87
  133.7 1.2 reshape.231
  134.9 13.3 %all-to-all-start.2 = ((f32[64,1,128]{2,1,0:T(1,128)}), f32[64,1,128]{2,1,0:T(1,128)S(1)}, u32[]{:S(2)}, u32[]{:S(2)}) async-start(f32[64,1,128]{2,1,0:T(1,128)} %reshape.231), calls=%async_computation.2 | async-start | bytes 65536 | tf_op jit(solution)/shard_map/all_to_all | solution.py:120
  148.3 13.3 %all-to-all-done.2 = f32[64,1,128]{2,1,0:T(1,128)S(1)} async-done(((f32[64,1,128]{2,1,0:T(1,128)}), f32[64,1,128]{2,1,0:T(1,128)S(1)}, u32[]{:S(2)}, u32[]{:S(2)}) %all-to-all-start.2) | async-done | bytes 32800 | tf_op jit(solution)/shard_map/all_to_all | solution.py:120
  164.1 1.2 gather_fusion.5
  165.3 6.5 %all-to-all-start.3 = ((f32[8,2,4]{2,1,0:T(2,128)}), f32[8,2,4]{2,1,0:T(2,128)S(1)}, u32[]{:S(2)}, u32[]{:S(2)}) async-start(f32[8,2,4]{2,1,0:T(2,128)} %gather_fusion.5), calls=%async_computation.3 | async-start | bytes 16384 | tf_op jit(solution)/shard_map/all_to_all | solution.py:133
  171.8 4.6 %all-to-all-done.3 = f32[8,2,4]{2,1,0:T(2,128)S(1)} async-done(((f32[8,2,4]{2,1,0:T(2,128)}), f32[8,2,4]{2,1,0:T(2,128)S(1)}, u32[]{:S(2)}, u32[]{:S(2)}) %all-to-all-start.3) | async-done | bytes 288 | tf_op jit(solution)/shard_map/all_to_all | solution.py:133
  (53 shorter events, 8.8 us)
Async XLA Ops:
  7.2 15.3 %copy-start = (s32[64]{0:T(128)S(1)}, s32[64]{0:T(128)}, u32[]{:S(2)}) copy-start(s32[64]{0:T(128)} %param.11) | copy-start | bytes 772
  7.2 52.0 %copy-start.1 = (bf16[776,1536]{1,0:T(8,128)(2,1)S(1)}, bf16[776,1536]{1,0:T(8,128)(2,1)}, u32[]{:S(2)}) copy-start(bf16[776,1536]{1,0:T(8,128)(2,1)} %param.9) | copy-start | bytes 7151620
  7.2 109.9 %all-gather.2.cloned.1.call-start = ((), (), s32[]{:S(2)}) async-start(), calls=%async_computation.4 | async-start | bytes 6684672 | tf_op jit(solution)/shard_map/all_gather | solution.py:72
  26.7 16.7 %all-to-all-start = ((s32[8,1,4]{2,1,0:T(1,128)}), s32[8,1,4]{2,1,0:T(1,128)S(1)}, u32[]{:S(2)}, u32[]{:S(2)}) async-start(s32[8,1,4]{2,1,0:T(1,128)} %bitcast.23), calls=%async_computation | async-start | bytes 8192 | tf_op jit(solution)/shard_map/all_to_all | solution.py:109
  44.7 31.5 %all-to-all-start.1 = ((s32[64,8,4]{1,2,0:T(4,128)}), s32[64,8,4]{1,2,0:T(4,128)S(1)}, u32[]{:S(2)}, u32[]{:S(2)}) async-start(s32[64,8,4]{1,2,0:T(4,128)} %broadcast_in_dim.39), calls=%async_computation.1 | async-start | bytes 262144 | tf_op jit(solution)/shard_map/all_to_all | solution.py:112
  134.9 26.7 %all-to-all-start.2 = ((f32[64,1,128]{2,1,0:T(1,128)}), f32[64,1,128]{2,1,0:T(1,128)S(1)}, u32[]{:S(2)}, u32[]{:S(2)}) async-start(f32[64,1,128]{2,1,0:T(1,128)} %reshape.231), calls=%async_computation.2 | async-start | bytes 65536 | tf_op jit(solution)/shard_map/all_to_all | solution.py:120
  165.3 11.1 %all-to-all-start.3 = ((f32[8,2,4]{2,1,0:T(2,128)}), f32[8,2,4]{2,1,0:T(2,128)S(1)}, u32[]{:S(2)}, u32[]{:S(2)}) async-start(f32[8,2,4]{2,1,0:T(2,128)} %gather_fusion.5), calls=%async_computation.3 | async-start | bytes 16384 | tf_op jit(solution)/shard_map/all_to_all | solution.py:133
Sparse Core Ops, SparseCore 0:
  21.1 95.9 all-gather.1

commit v4 on v3

--- a/solution.py
+++ b/solution.py
@@ -15,6 +15,17 @@
 def stats_kernel(offset_ref, rows_ref, emb_ref, marks_ref, out_ref):
     logits = jnp.dot(rows_ref[...], emb_ref[...], preferred_element_type=jnp.float32)
     columns = offset_ref[0] + lax.broadcasted_iota(jnp.int32, logits.shape, 1)
+    write_stats(logits, columns, marks_ref, out_ref)
+
+
+def ids_kernel(ids_ref, rows_ref, emb_ref, marks_ref, out_ref):
+    logits = lax.dot_general(
+        rows_ref[...], emb_ref[...], (((1,), (1,)), ((), ())), preferred_element_type=jnp.float32
+    )
+    write_stats(logits, ids_ref[...], marks_ref, out_ref)
+
+
+def write_stats(logits, columns, marks_ref, out_ref):
     usable = columns < VREAL
     maximum = jnp.max(jnp.where(usable, logits, -jnp.inf), axis=1, keepdims=True)
     weights = jnp.where(usable, jnp.exp(logits - maximum), 0.0)
@@ -46,6 +57,122 @@
     )(offset.reshape(1), rows, emb_t, marks.reshape(n, 1))
 
 
+def id_stats(rows, table, ids, marks):
+    n, d = rows.shape
+    v = table.shape[0]
+    block = ROW_BLOCK if n % ROW_BLOCK == 0 else n
+    return pl.pallas_call(
+        ids_kernel,
+        grid=(n // block,),
+        in_specs=[
+            pl.BlockSpec((1, v), lambda i: (0, 0)),
+            pl.BlockSpec((block, d), lambda i: (i, 0)),
+            pl.BlockSpec((v, d), lambda i: (0, 0)),
+            pl.BlockSpec((block, 1), lambda i: (i, 0)),
+        ],
+        out_specs=pl.BlockSpec((block, 4), lambda i: (i, 0)),
+        out_shape=jax.ShapeDtypeStruct((n, 4), jnp.float32),
+        cost_estimate=pl.CostEstimate(
+            flops=2 * n * v * d, transcendentals=n * v, bytes_accessed=2 * (n + v) * d + 20 * n
+        ),
+        interpret=INTERPRET,
+    )(ids.reshape(1, v), rows, table, marks.reshape(n, 1))
+
+
+def merge_stats(parts, axis):
+    part_max, part_tot, part_wt, part_ch = [lax.index_in_dim(parts, i, axis=-1, keepdims=False) for i in range(4)]
+    overall = jnp.max(part_max, axis=axis, keepdims=True)
+    factor = jnp.exp(part_max - overall)
+    return jnp.stack([
+        jnp.squeeze(overall, axis),
+        jnp.sum(part_tot * factor, axis=axis),
+        jnp.sum(part_wt * factor, axis=axis),
+        jnp.sum(part_ch, axis=axis),
+    ], axis=-1)
+
+
+def plane_fn(sizes):
+    n_ty, n_tc, n_tx, n_tz = sizes
+    dp_axes = ("ty", "tc")
+
+    def local(hidden, norm_gain, embedding, targets, lengths, loss_mask, deal_slots):
+        group_rank = lax.axis_index("ty") * n_tc + lax.axis_index("tc")
+        core = lax.axis_index("tc")
+        xr, zr = lax.axis_index("tx"), lax.axis_index("tz")
+        sequences, row_width = hidden.shape[0], hidden.shape[1]
+        vocab_rows, width = embedding.shape
+
+        half = vocab_rows // n_tc
+        mine = lax.dynamic_slice_in_dim(embedding, core * half, half, 0)
+        fetched, sources = [], []
+        for step in range(1, n_tx // 2 + 1):
+            if 2 * step == n_tx:
+                quarter = half // 2
+                fetched.append(lax.ppermute(mine[:quarter], "tx", [(i, (i + step) % n_tx) for i in range(n_tx)]))
+                fetched.append(lax.ppermute(mine[quarter:], "tx", [(i, (i - step) % n_tx) for i in range(n_tx)]))
+                sources.append((-step, 0, quarter))
+                sources.append((step, quarter, half))
+            else:
+                fetched.append(lax.ppermute(mine, "tx", [(i, (i + step) % n_tx) for i in range(n_tx)]))
+                fetched.append(lax.ppermute(mine, "tx", [(i, (i - step) % n_tx) for i in range(n_tx)]))
+                sources.append((-step, 0, half))
+                sources.append((step, 0, half))
+        got = jnp.concatenate(fetched, 0)
+        other = lax.ppermute(got, "tc", [(i, (i + 1) % n_tc) for i in range(n_tc)]) if n_tc == 2 else None
+        got_ids = []
+        for shift, lo, hi in sources:
+            rank = ((xr + shift) % n_tx) * n_tz + zr
+            got_ids.append(rank * vocab_rows + jnp.arange(lo, hi, dtype=jnp.int32))
+        got_ids = jnp.concatenate(got_ids)
+        mine_ids = got_ids + core * half
+        other_ids = got_ids + (1 - core) * half
+
+        owned_seqs = group_rank * sequences + jnp.arange(sequences, dtype=jnp.int32)
+        destination = deal_slots[owned_seqs] // sequences
+        send_order = jnp.argsort(destination, stable=True)
+        every_group = deal_slots // sequences
+        arrived = jnp.argsort((every_group != group_rank).astype(jnp.int32), stable=True)[:sequences]
+        arrived_slot = deal_slots[arrived] % sequences
+        positions = (xr * n_tz + zr) * row_width + jnp.arange(row_width, dtype=jnp.int32)
+        scored = (positions[None, :] < lengths[owned_seqs][:, None]) & (loss_mask == 1)
+        marked = jnp.where(scored, targets, -1)
+        undo_order = jnp.argsort(send_order)
+
+        normed = normalize(hidden, norm_gain)
+        row_block = lax.all_gather(normed, "tz", axis=1, tiled=True)
+
+        came = lax.all_to_all(marked[send_order], dp_axes, split_axis=0, concat_axis=0, tiled=True)
+        worker_marks = came[jnp.argsort(arrived_slot)]
+        spread = jnp.broadcast_to(worker_marks[None], (n_tz,) + worker_marks.shape)
+        block_marks = lax.all_to_all(spread, "tz", split_axis=0, concat_axis=0, tiled=True)
+        block_marks = jnp.transpose(block_marks, (0, 2, 1)).reshape(-1)
+
+        flat_rows = jnp.transpose(row_block, (1, 0, 2)).reshape(-1, width)
+        own_ids = (xr * n_tz + zr) * vocab_rows + jnp.arange(vocab_rows, dtype=jnp.int32)
+        parts = [
+            id_stats(flat_rows, embedding, own_ids, block_marks),
+            id_stats(flat_rows, got, mine_ids, block_marks),
+        ]
+        if other is not None:
+            parts.append(id_stats(flat_rows, other, other_ids, block_marks))
+        local_stats = merge_stats(jnp.stack(parts), 0)
+
+        stats = jnp.transpose(local_stats.reshape(n_tz, row_width, sequences, 4), (0, 3, 2, 1))
+        parts = lax.all_to_all(stats, "tz", split_axis=0, concat_axis=0, tiled=True)
+        merged = merge_stats(jnp.transpose(parts, (0, 2, 3, 1)), 0)
+        overall, totals, weighted, chosen = [merged[..., i] for i in range(4)]
+        log_total = overall + jnp.log(totals)
+        usable_rows = worker_marks >= 0
+        log_prob = jnp.where(usable_rows, chosen - log_total, 0.0)
+        entropy = jnp.where(usable_rows, log_total - weighted / totals, 0.0)
+
+        both = jnp.stack([log_prob, entropy], axis=1)[arrived_slot]
+        returned = lax.all_to_all(both, dp_axes, split_axis=0, concat_axis=0, tiled=True)[undo_order]
+        return returned[:, 0], returned[:, 1]
+
+    return local
+
+
 def normalize(hidden, norm_gain):
     values = hidden.astype(jnp.float32)
     inverse = lax.rsqrt(jnp.mean(values * values, axis=2, keepdims=True) + 1e-05)
@@ -136,8 +263,35 @@
     return local
 
 
+PLANE = True
+EMBEDDING_ROWS = 49664
+
+
+def embedding_halves(mesh):
+    rows = EMBEDDING_ROWS // mesh.shape["tensor"]
+    return EMBEDDING_ROWS % mesh.shape["tensor"] == 0 and rows % 4 == 0
+
+
+def split_dp(mesh):
+    col = mesh.devices[:, 0]
+    cores = len({getattr(d, "core_on_chip", 0) for d in col})
+    if cores != 2 or col.size % cores:
+        return None
+    return col.size // cores, cores
+
+
 def solution(mesh):
     split = split_tensor(mesh)
+    cores = split_dp(mesh)
+    if PLANE and split is not None and cores is not None and embedding_halves(mesh):
+        sizes = (cores[0], cores[1], split[0], split[1])
+        run_mesh = Mesh(mesh.devices.reshape(sizes), ("ty", "tc", "tx", "tz"))
+        dp, tensor = ("ty", "tc"), ("tx", "tz")
+        placed = (P(dp, tensor, None), P(), P(tensor, None), P(dp, tensor), P(), P(dp, tensor), P())
+        return jax.shard_map(
+            plane_fn(sizes), mesh=run_mesh, in_specs=placed,
+            out_specs=(P(dp, tensor), P(dp, tensor)), check_vma=False,
+        )
     if split is None:
         run_mesh, tensor_axes, tensor_size = mesh, ("tensor",), (mesh.shape["tensor"],)
     else:

time: 186 us -> 200 us (1.075)
  local copies, waits for them, and re-layouts: 19.9 us -> 37.2 us
  blocking collectives: 11.5 us -> 0 us
  Pallas kernels: 13.8 us -> 18.2 us
  waiting for transfers between devices: 70.7 us -> 73 us
  starting transfers between devices: 46 us -> 48 us
    ppermute x0 -> x5, waiting for transfers between devices: none -> 45 us  [the longest x1 31.9 us: local(): lax.ppermute(mine[quarter:], 'tx', [(i, (i - step) % n_tx) for i in range...]
    all_gather x1, waiting for transfers between devices: 39.5 us -> 0.01 us  [local(): row_block = lax.all_gather(normed, 'tz', axis=1, tiled=True)]
    concatenate x0 -> x2, local copies, waits for them, and re-layouts: none -> 19.5 us  [the longest x1 19.4 us: local(): got = jnp.concatenate(fetched, 0)]
    ppermute x0 -> x5, starting transfers between devices: none -> 18.6 us  [the longest x1 5.19 us: local(): lax.ppermute(mine, 'tx', [(i, (i - step) % n_tx) for i in range(n_tx)])]
    all_to_all x4, starting transfers between devices: 46 us -> 29.4 us  [the longest x1 14.9 us: local(): lax.all_to_all(spread, 'tz', split_axis=0, concat_axis=0, tiled=True)]
    all_gather x1 -> x0, blocking collectives: 11.5 us -> none  [gather_rows(): rows = lax.all_gather(rows, name, axis=1, tiled=True)]
    unnamed x9 -> x18, local copies, waits for them, and re-layouts: 6.16 us -> 1.15 us
    pallas_call x1 -> x3, Pallas kernels: 13.8 us -> 18.2 us  [id_stats(): pl.pallas_call(ids_kernel, grid=(n // block,), in_specs=[pl.BlockSpec((1,...]
  transfers between devices with their start and end apart: 5 -> 10, of which waited for: 4 -> 6; matrix products, arithmetic and copies ran while one was open for 9% -> 18% of each run, Pallas kernels for 0% -> 6%
where the time goes in v4:
time: 200 us; the launch traced here: 199 us
  waiting for transfers between devices  73 us (36%)
  starting transfers between devices  48 us (24%)
  local copies, waits for them, and re-layouts  37.2 us (19%)
  Pallas kernels  18.2 us (9%)
  between operations  14.4 us (7%)
  other arithmetic  8.23 us (4%)
    ppermute x1, waiting for transfers between devices, local(): lax.ppermute(mine[quarter:], 'tx', [(i, (i - step) % n_tx) for i in range...  31.9 us
    concatenate x1, local copies, waits for them, and re-layouts, local(): got = jnp.concatenate(fetched, 0)  19.4 us
    pallas_call x3, Pallas kernels, id_stats(): pl.pallas_call(ids_kernel, grid=(n // block,), in_specs=[pl.BlockSpec((1,...  18.2 us
    all_to_all x1, starting transfers between devices, local(): lax.all_to_all(spread, 'tz', split_axis=0, concat_axis=0, tiled=True)  14.9 us
    ppermute x1, waiting for transfers between devices, local(): lax.ppermute(mine[:quarter], 'tx', [(i, (i + step) % n_tx) for i in range...  13.2 us
    all_to_all x1, waiting for transfers between devices, local(): parts = lax.all_to_all(stats, 'tz', split_axis=0, concat_axis=0, tiled=True)  11.2 us
    all_to_all x1, waiting for transfers between devices, local(): lax.all_to_all(spread, 'tz', split_axis=0, concat_axis=0, tiled=True)  10.9 us
    all_to_all x1, starting transfers between devices, local(): lax.all_to_all(both, dp_axes, split_axis=0, concat_axis=0, tiled=True)  6.41 us
  transfers between devices with their start and end apart: 10, of which 6 were waited for; matrix products, arithmetic and copies ran while one was open for 18% of the time, Pallas kernels for 6%

profile of v4, /device:TPU:1, one launch (start us, length us, event | category | flops | bytes accessed | tf_op | source)
XLA Modules:
  0.0 199.0 jit_solution(9646511395726604456)
XLA Ops:
  7.3 2.7 %constant_dynamic-slice_fusion.2 = bf16[388,1536]{1,0:T(8,128)(2,1)} fusion(bf16[776,1536]{1,0:T(8,128)(2,1)} %emb_ref.1, s32[]{:T(128)S(6)} %select_n.123), kind=kLoop, calls=%fused_computation.74 | loop fusion | bytes 2383876 | tf_op jit(solution)/shard_map/dynamic_slice | solution.py:106
  10.0 5.2 %collective-permute-start.1 = (bf16[388,1536]{1,0:T(8,128)(2,1)}, bf16[388,1536]{1,0:T(8,128)(2,1)}, u32[]{:S(2)}, u32[]{:S(2)}) collective-permute-start(bf16[388,1536]{1,0:T(8,128)(2,1)} %constant_dynamic-slice_fusion.2), channel_id=1, source_target_pairs={{0,48},{16,0},{32,16},{48,32},{1,49},{17,1},{33,17},{49,33},{2,50}... | collective-permute-start | bytes 3575816 | tf_op jit(solution)/shard_map/ppermute | solution.py:117
  15.2 1.9 collective-permute-start
  17.1 1.1 constant_dynamic-slice_fusion
  18.3 3.6 %collective-permute-start.3 = (bf16[194,1536]{1,0:T(8,128)(2,1)}, bf16[194,1536]{1,0:T(8,128)(2,1)S(1)}, u32[]{:S(2)}, u32[]{:S(2)}) collective-permute-start(bf16[194,1536]{1,0:T(8,128)(2,1)} %get-tuple-element.20), channel_id=1, source_target_pairs={{0,32},{16,48},{32,0},{48,16},{1,33},{17,49},{33,1},{49,17},{2,34}... | collective-permute-start | bytes 1787912 | tf_op jit(solution)/shard_map/ppermute | solution.py:112
  21.9 3.2 %collective-permute-start.2 = (bf16[194,1536]{1,0:T(8,128)(2,1)S(1)}, bf16[194,1536]{1,0:T(8,128)(2,1)S(1)}, u32[]{:S(2)}, u32[]{:S(2)}) collective-permute-start(bf16[194,1536]{1,0:T(8,128)(2,1)S(1)} %get-tuple-element.21), channel_id=1, source_target_pairs={{0,32},{16,48},{32,0},{48,16},{1,33},{17,49},{33,1},{49,17},{2,34}... | collective-permute-start | bytes 1787912 | tf_op jit(solution)/shard_map/ppermute | solution.py:111
  26.0 31.9 %collective-permute-done.3 = bf16[194,1536]{1,0:T(8,128)(2,1)S(1)} collective-permute-done((bf16[194,1536]{1,0:T(8,128)(2,1)}, bf16[194,1536]{1,0:T(8,128)(2,1)S(1)}, u32[]{:S(2)}, u32[]{:S(2)}) %collective-permute-start.3) | collective-permute-done | bytes 596000 | tf_op jit(solution)/shard_map/ppermute | solution.py:112
  57.9 13.2 %collective-permute-done.2 = bf16[194,1536]{1,0:T(8,128)(2,1)S(1)} collective-permute-done((bf16[194,1536]{1,0:T(8,128)(2,1)S(1)}, bf16[194,1536]{1,0:T(8,128)(2,1)S(1)}, u32[]{:S(2)}, u32[]{:S(2)}) %collective-permute-start.2) | collective-permute-done | bytes 596000 | tf_op jit(solution)/shard_map/ppermute | solution.py:111
  71.0 19.4 %concatenate.34.emb_ref = bf16[1164,1536]{1,0:T(8,128)(2,1)} concatenate(bf16[388,1536]{1,0:T(8,128)(2,1)} %collective-permute-done, bf16[388,1536]{1,0:T(8,128)(2,1)} %collective-permute-done.1, bf16[194,1536]{1,0:T(8,128)(2,1)S(1)} %collective-permute-done.2, bf16[194,1536]{1,0:T(8,128)(2,1)S(1)} %collective-permute-done.3), dimensions={0} | concatenate | bytes 7151616 | tf_op jit(solution)/shard_map/concatenate | solution.py:120
  90.4 4.7 %collective-permute-start.4 = (bf16[1164,1536]{1,0:T(8,128)(2,1)}, bf16[1164,1536]{1,0:T(8,128)(2,1)}, u32[]{:S(2)}, u32[]{:S(2)}) collective-permute-start(bf16[1164,1536]{1,0:T(8,128)(2,1)} %concatenate.34.emb_ref), channel_id=1, source_target_pairs={{0,64},{64,0},{1,65},{65,1},{2,66},{66,2},{3,67},{67,3},{4,68},{68... | collective-permute-start | bytes 10727432 | tf_op jit(solution)/shard_map/ppermute | solution.py:121
  96.6 2.0 %sort.66 = (s32[64]{0:T(128)}, s32[64]{0:T(128)S(1)}) sort(s32[64]{0:T(128)S(1)} %compare_convert_fusion, s32[64]{0:T(128)S(1)} %iota.43), dimensions={0}, to_apply=%region_1.2 | sort | flops 384 | bytes 1024 | tf_op jit(solution)/shard_map/jit(argsort)/sort | solution.py:134
  99.7 1.1 gather_fusion.2
  100.9 4.6 %all-to-all-start = ((s32[8,1,4]{2,1,0:T(1,128)}), s32[8,1,4]{2,1,0:T(1,128)S(1)}, u32[]{:S(2)}, u32[]{:S(2)}) async-start(s32[8,1,4]{2,1,0:T(1,128)} %bitcast.25), calls=%async_computation | async-start | bytes 8192 | tf_op jit(solution)/shard_map/all_to_all | solution.py:144
  108.8 1.2 all-to-all-done
  111.3 14.9 %all-to-all-start.1 = ((s32[16,8,4]{1,2,0:T(4,128)}), s32[16,8,4]{1,2,0:T(4,128)S(1)}, u32[]{:S(2)}, u32[]{:S(2)}) async-start(s32[16,8,4]{1,2,0:T(4,128)} %broadcast_in_dim.40), calls=%async_computation.1 | async-start | bytes 65536 | tf_op jit(solution)/shard_map/all_to_all | solution.py:147
  126.8 10.9 %all-to-all-done.1 = s32[16,8,4]{1,2,0:T(4,128)S(1)} async-done(((s32[16,8,4]{1,2,0:T(4,128)}), s32[16,8,4]{1,2,0:T(4,128)S(1)}, u32[]{:S(2)}, u32[]{:S(2)}) %all-to-all-start.1) | async-done | bytes 2080 | tf_op jit(solution)/shard_map/all_to_all | solution.py:147
  138.5 5.4 %shard_map.86 = f32[512,4]{1,0:T(8,128)} custom-call(s32[1,776]{1,0:T(1,128)} %iota_add_fusion.ids_ref, bf16[512,1536]{1,0:T(8,128)(2,1)} %bitcast.88, bf16[776,1536]{1,0:T(8,128)(2,1)} %emb_ref.1, s32[512,1]{1,0:T(8,128)} %reshape_reshape.6.marks_ref), custom_call_target="tpu_custom_call" | custom-call | flops 1220542464 | bytes 3966976 | tf_op jit(solution)/shard_map/pallas_call | solution.py:64
  145.0 6.4 %shard_map.87 = f32[512,4]{1,0:T(8,128)} custom-call(s32[1,1164]{1,0:T(1,128)} %get-tuple-element.27.ids_ref, bf16[512,1536]{1,0:T(8,128)(2,1)} %bitcast.89, bf16[1164,1536]{1,0:T(8,128)(2,1)} %concatenate.34.emb_ref, s32[512,1]{1,0:T(8,128)} %reshape_reshape.6.marks_ref), custom_call_target="tpu_custom_call" | custom-call | flops 1830813696 | bytes 5158912 | tf_op jit(solution)/shard_map/pallas_call | solution.py:64
  152.4 6.4 %shard_map.88 = f32[512,4]{1,0:T(8,128)} custom-call(s32[1,1164]{1,0:T(1,128)} %get-tuple-element.28.ids_ref, bf16[512,1536]{1,0:T(8,128)(2,1)} %bitcast.90, bf16[1164,1536]{1,0:T(8,128)(2,1)} %collective-permute-done.4.emb_ref, s32[512,1]{1,0:T(8,128)} %reshape_reshape.6.marks_ref), custom_call_target="tpu_custom_call" | custom-call | flops 1830813696 | bytes 5158912 | tf_op jit(solution)/shard_map/pallas_call | solution.py:64
  161.2 3.5 %all-to-all-start.2 = ((f32[16,1,128]{2,1,0:T(1,128)}), f32[16,1,128]{2,1,0:T(1,128)S(1)}, u32[]{:S(2)}, u32[]{:S(2)}) async-start(f32[16,1,128]{2,1,0:T(1,128)} %reshape.309), calls=%async_computation.2 | async-start | bytes 16384 | tf_op jit(solution)/shard_map/all_to_all | solution.py:161
  164.7 11.2 %all-to-all-done.2 = f32[16,1,128]{2,1,0:T(1,128)S(1)} async-done(((f32[16,1,128]{2,1,0:T(1,128)}), f32[16,1,128]{2,1,0:T(1,128)S(1)}, u32[]{:S(2)}, u32[]{:S(2)}) %all-to-all-start.2) | async-done | bytes 8224 | tf_op jit(solution)/shard_map/all_to_all | solution.py:161
  178.1 1.2 gather_fusion.5
  179.3 6.4 %all-to-all-start.3 = ((f32[8,2,4]{2,1,0:T(2,128)}), f32[8,2,4]{2,1,0:T(2,128)S(1)}, u32[]{:S(2)}, u32[]{:S(2)}) async-start(f32[8,2,4]{2,1,0:T(2,128)} %gather_fusion.5), calls=%async_computation.3 | async-start | bytes 16384 | tf_op jit(solution)/shard_map/all_to_all | solution.py:170
  185.7 4.6 %all-to-all-done.3 = f32[8,2,4]{2,1,0:T(2,128)S(1)} async-done(((f32[8,2,4]{2,1,0:T(2,128)}), f32[8,2,4]{2,1,0:T(2,128)S(1)}, u32[]{:S(2)}, u32[]{:S(2)}) %all-to-all-start.3) | async-done | bytes 288 | tf_op jit(solution)/shard_map/all_to_all | solution.py:170
  (91 shorter events, 17.9 us)
Async XLA Ops:
  7.2 88.6 %copy-start = (s32[64]{0:T(128)S(1)}, s32[64]{0:T(128)}, u32[]{:S(2)}) copy-start(s32[64]{0:T(128)} %param.11) | copy-start | bytes 772
  7.2 10.0 %copy-start.2 = (bf16[776,1536]{1,0:T(8,128)(2,1)S(1)}, bf16[776,1536]{1,0:T(8,128)(2,1)}, u32[]{:S(2)}) copy-start(bf16[776,1536]{1,0:T(8,128)(2,1)} %emb_ref.1) | copy-start | bytes 7151620
  7.2 131.3 %all-gather.2.cloned.1.call-start = ((), (), s32[]{:S(2)}) async-start(), calls=%async_computation.4 | async-start | bytes 1671168 | tf_op jit(solution)/shard_map/all_gather | solution.py:142
  7.2 17.8 %copy-start.3 = (bf16[8,4,1536]{2,1,0:T(4,128)(2,1)S(1)}, bf16[8,4,1536]{2,1,0:T(4,128)(2,1)}, u32[]{:S(2)}) copy-start(bf16[8,4,1536]{2,1,0:T(4,128)(2,1)} %param.7) | copy-start | bytes 294916
  7.3 17.9 %copy-start.4 = (f32[1536]{0:T(1024)S(1)}, f32[1536]{0:T(1024)}, u32[]{:S(2)}) copy-start(f32[1536]{0:T(1024)} %param.8) | copy-start | bytes 18436
  10.0 61.0 %collective-permute-start.1 = (bf16[388,1536]{1,0:T(8,128)(2,1)}, bf16[388,1536]{1,0:T(8,128)(2,1)}, u32[]{:S(2)}, u32[]{:S(2)}) collective-permute-start(bf16[388,1536]{1,0:T(8,128)(2,1)} %constant_dynamic-slice_fusion.2), channel_id=1, source_target_pairs={{0,48},{16,0},{32,16},{48,32},{1,49},{17,1},{33,17},{49,33},{2,50}... | collective-permute-start | bytes 3575816 | tf_op jit(solution)/shard_map/ppermute | solution.py:117
  15.2 55.8 %collective-permute-start = (bf16[388,1536]{1,0:T(8,128)(2,1)}, bf16[388,1536]{1,0:T(8,128)(2,1)}, u32[]{:S(2)}, u32[]{:S(2)}) collective-permute-start(bf16[388,1536]{1,0:T(8,128)(2,1)} %constant_dynamic-slice_fusion.2), channel_id=1, source_target_pairs={{0,16},{16,32},{32,48},{48,0},{1,17},{17,33},{33,49},{49,1},{2,18}... | collective-permute-start | bytes 3575816 | tf_op jit(solution)/shard_map/ppermute | solution.py:116
  18.3 39.6 %collective-permute-start.3 = (bf16[194,1536]{1,0:T(8,128)(2,1)}, bf16[194,1536]{1,0:T(8,128)(2,1)S(1)}, u32[]{:S(2)}, u32[]{:S(2)}) collective-permute-start(bf16[194,1536]{1,0:T(8,128)(2,1)} %get-tuple-element.20), channel_id=1, source_target_pairs={{0,32},{16,48},{32,0},{48,16},{1,33},{17,49},{33,1},{49,17},{2,34}... | collective-permute-start | bytes 1787912 | tf_op jit(solution)/shard_map/ppermute | solution.py:112
  21.9 49.1 %collective-permute-start.2 = (bf16[194,1536]{1,0:T(8,128)(2,1)S(1)}, bf16[194,1536]{1,0:T(8,128)(2,1)S(1)}, u32[]{:S(2)}, u32[]{:S(2)}) collective-permute-start(bf16[194,1536]{1,0:T(8,128)(2,1)S(1)} %get-tuple-element.21), channel_id=1, source_target_pairs={{0,32},{16,48},{32,0},{48,16},{1,33},{17,49},{33,1},{49,17},{2,34}... | collective-permute-start | bytes 1787912 | tf_op jit(solution)/shard_map/ppermute | solution.py:111
  26.0 69.2 %copy-start.1 = (s32[64]{0:T(128)S(1)}, s32[64]{0:T(128)}, u32[]{:S(2)}) copy-start(s32[64]{0:T(128)} %param.13) | copy-start | bytes 772
  26.0 70.5 %copy-start.5 = (s32[8,4]{0,1:T(4,128)S(1)}, s32[8,4]{0,1:T(4,128)}, u32[]{:S(2)}) copy-start(s32[8,4]{0,1:T(4,128)} %param.10) | copy-start | bytes 388
  26.0 70.5 %copy-start.6 = (s32[8,4]{0,1:T(4,128)S(1)}, s32[8,4]{0,1:T(4,128)}, u32[]{:S(2)}) copy-start(s32[8,4]{0,1:T(4,128)} %param.12) | copy-start | bytes 388
  90.4 62.0 %collective-permute-start.4 = (bf16[1164,1536]{1,0:T(8,128)(2,1)}, bf16[1164,1536]{1,0:T(8,128)(2,1)}, u32[]{:S(2)}, u32[]{:S(2)}) collective-permute-start(bf16[1164,1536]{1,0:T(8,128)(2,1)} %concatenate.34.emb_ref), channel_id=1, source_target_pairs={{0,64},{64,0},{1,65},{65,1},{2,66},{66,2},{3,67},{67,3},{4,68},{68... | collective-permute-start | bytes 10727432 | tf_op jit(solution)/shard_map/ppermute | solution.py:121
  100.9 9.2 %all-to-all-start = ((s32[8,1,4]{2,1,0:T(1,128)}), s32[8,1,4]{2,1,0:T(1,128)S(1)}, u32[]{:S(2)}, u32[]{:S(2)}) async-start(s32[8,1,4]{2,1,0:T(1,128)} %bitcast.25), calls=%async_computation | async-start | bytes 8192 | tf_op jit(solution)/shard_map/all_to_all | solution.py:144
  111.3 26.4 %all-to-all-start.1 = ((s32[16,8,4]{1,2,0:T(4,128)}), s32[16,8,4]{1,2,0:T(4,128)S(1)}, u32[]{:S(2)}, u32[]{:S(2)}) async-start(s32[16,8,4]{1,2,0:T(4,128)} %broadcast_in_dim.40), calls=%async_computation.1 | async-start | bytes 65536 | tf_op jit(solution)/shard_map/all_to_all | solution.py:147
  161.2 14.8 %all-to-all-start.2 = ((f32[16,1,128]{2,1,0:T(1,128)}), f32[16,1,128]{2,1,0:T(1,128)S(1)}, u32[]{:S(2)}, u32[]{:S(2)}) async-start(f32[16,1,128]{2,1,0:T(1,128)} %reshape.309), calls=%async_computation.2 | async-start | bytes 16384 | tf_op jit(solution)/shard_map/all_to_all | solution.py:161
  179.3 11.1 %all-to-all-start.3 = ((f32[8,2,4]{2,1,0:T(2,128)}), f32[8,2,4]{2,1,0:T(2,128)S(1)}, u32[]{:S(2)}, u32[]{:S(2)}) async-start(f32[8,2,4]{2,1,0:T(2,128)} %gather_fusion.5), calls=%async_computation.3 | async-start | bytes 16384 | tf_op jit(solution)/shard_map/all_to_all | solution.py:170
Sparse Core Ops, SparseCore 0:
  26.1 68.5 all-gather.1

commit v5 on v3

--- a/solution.py
+++ b/solution.py
@@ -9,17 +9,19 @@
 
 VREAL = 49155
 INTERPRET = False
-ROW_BLOCK = 256
+ROW_BLOCK = 512
 
 
 def stats_kernel(offset_ref, rows_ref, emb_ref, marks_ref, out_ref):
     logits = jnp.dot(rows_ref[...], emb_ref[...], preferred_element_type=jnp.float32)
-    columns = offset_ref[0] + lax.broadcasted_iota(jnp.int32, logits.shape, 1)
-    usable = columns < VREAL
-    maximum = jnp.max(jnp.where(usable, logits, -jnp.inf), axis=1, keepdims=True)
-    weights = jnp.where(usable, jnp.exp(logits - maximum), 0.0)
+    columns = offset_ref[0] + lax.broadcasted_iota(jnp.int32, (1, logits.shape[1]), 1)
+    bias = jnp.where(columns < VREAL, 0.0, -jnp.inf)
+    masked = logits + bias
+    maximum = jnp.max(masked, axis=1, keepdims=True)
+    shift = jnp.maximum(maximum, jnp.finfo(jnp.float32).min)
+    weights = jnp.exp(masked - shift)
     totals = jnp.sum(weights, axis=1, keepdims=True)
-    weighted = jnp.sum(weights * jnp.where(usable, logits, 0.0), axis=1, keepdims=True)
+    weighted = jnp.sum(weights * logits, axis=1, keepdims=True)
     chosen = jnp.sum(jnp.where(columns == marks_ref[...], logits, 0.0), axis=1, keepdims=True)
     out_ref[...] = jnp.concatenate([maximum, totals, weighted, chosen], axis=1)
 

time: 186 us -> 185 us (level)
  no operation moved by 1% of the time
where the time goes in v5:
time: 185 us; the launch traced here: 184 us
  waiting for transfers between devices  70.7 us (38%)
  starting transfers between devices  46 us (25%)
  local copies, waits for them, and re-layouts  19.9 us (11%)
  between operations  14.2 us (8%)
  Pallas kernels  12.8 us (7%)
  blocking collectives  11.5 us (6%)
  other arithmetic  8.94 us (5%)
    all_gather x1, waiting for transfers between devices, gather_rows(): rows = lax.all_gather(rows, name, axis=1, tiled=True)  39.5 us
    all_to_all x1, starting transfers between devices, local(): lax.all_to_all(spread, tensor_axes, split_axis=0, concat_axis=0, tiled=True)  14.4 us
    all_to_all x1, starting transfers between devices, local(): lax.all_to_all(stats, tensor_axes, split_axis=0, concat_axis=0, tiled=True)  13.3 us
    all_to_all x1, waiting for transfers between devices, local(): lax.all_to_all(stats, tensor_axes, split_axis=0, concat_axis=0, tiled=True)  13.3 us
    all_to_all x1, waiting for transfers between devices, local(): lax.all_to_all(spread, tensor_axes, split_axis=0, concat_axis=0, tiled=True)  13.3 us
    pallas_call x1, Pallas kernels, row_stats(): pl.pallas_call(stats_kernel, grid=(n // block,), in_specs=[pl.BlockSpec(m...  12.8 us
    all_to_all x1, starting transfers between devices, local(): lax.all_to_all(marked[send_order], 'dp', split_axis=0, concat_axis=0, til...  11.7 us
    all_gather x1, blocking collectives, gather_rows(): rows = lax.all_gather(rows, name, axis=1, tiled=True)  11.5 us
  transfers between devices with their start and end apart: 5, of which 4 were waited for; matrix products, arithmetic and copies ran while one was open for 9% of the time, Pallas kernels for 0%

profile of v5, /device:TPU:1, one launch (start us, length us, event | category | flops | bytes accessed | tf_op | source)
XLA Modules:
  0.0 184.2 jit_solution(6587704738003980042)
XLA Ops:
  7.2 1.2 fusion
  8.4 1.0 fusion.2
  9.4 11.5 %all_gather.6 = bf16[8,16,1536]{2,0,1:T(8,128)(2,1)} all-gather(bf16[8,4,1536]{2,0,1:T(8,128)(2,1)S(1)} %fusion.2), channel_id=1, replica_groups=mesh['dp'=8,'tx'=4,'tz'=16] {'tx'}, dimensions={1}, use_global_device_ids=true | all-gather | bytes 491520 | tf_op jit(solution)/shard_map/all_gather | solution.py:74
  23.2 1.3 gather_fusion.1
  24.5 1.0 sort.65
  25.5 1.1 gather_fusion.2
  26.7 11.7 %all-to-all-start = ((s32[8,1,4]{2,1,0:T(1,128)}), s32[8,1,4]{2,1,0:T(1,128)S(1)}, u32[]{:S(2)}, u32[]{:S(2)}) async-start(s32[8,1,4]{2,1,0:T(1,128)} %bitcast.23), calls=%async_computation | async-start | bytes 8192 | tf_op jit(solution)/shard_map/all_to_all | solution.py:111
  39.1 2.0 %sort.66 = (s32[64]{0:T(128)}, s32[64]{0:T(128)S(1)}) sort(s32[64]{0:T(128)S(1)} %compare_convert_fusion, s32[64]{0:T(128)S(1)} %iota.27), dimensions={0}, to_apply=%region_1.2 | sort | flops 384 | bytes 1024 | tf_op jit(solution)/shard_map/jit(argsort)/sort | solution.py:101
  41.1 1.3 gather_fusion.3
  42.4 1.0 sort.67
  44.7 14.4 %all-to-all-start.1 = ((s32[64,8,4]{1,2,0:T(4,128)}), s32[64,8,4]{1,2,0:T(4,128)S(1)}, u32[]{:S(2)}, u32[]{:S(2)}) async-start(s32[64,8,4]{1,2,0:T(4,128)} %broadcast_in_dim.39), calls=%async_computation.1 | async-start | bytes 262144 | tf_op jit(solution)/shard_map/all_to_all | solution.py:114
  59.2 2.8 %copy.74 = bf16[776,1536]{0,1:T(8,128)(2,1)} copy(bf16[776,1536]{1,0:T(8,128)(2,1)S(1)} %copy-done.1) | data formatting | bytes 4767744 | tf_op args[2]
  62.0 1.0 sort.68
  63.0 13.3 %all-to-all-done.1 = s32[64,8,4]{1,2,0:T(4,128)S(1)} async-done(((s32[64,8,4]{1,2,0:T(4,128)}), s32[64,8,4]{1,2,0:T(4,128)S(1)}, u32[]{:S(2)}, u32[]{:S(2)}) %all-to-all-start.1) | async-done | bytes 8224 | tf_op jit(solution)/shard_map/all_to_all | solution.py:114
  76.3 1.3 reshape_reshape.4.marks_ref
  77.6 39.5 %all-gather.2.cloned.1.call-done = bf16[8,256,1536]{2,0,1:T(8,128)(2,1)} async-done(((bf16[8,16,1536]{2,0,1:T(8,128)(2,1)}), bf16[8,256,1536]{2,0,1:T(8,128)(2,1)}) %all-gather.2.cloned.1.call-update) | async-done | bytes 6291472 | tf_op jit(solution)/shard_map/all_gather | solution.py:74
  117.1 12.8 %shard_map.86 = f32[2048,4]{1,0:T(8,128)} custom-call(s32[1]{0:T(128)} %bitcast.3.offset_ref, bf16[2048,1536]{1,0:T(8,128)(2,1)} %bitcast.73, bf16[1536,776]{1,0:T(8,128)(2,1)} %bitcast.61, s32[2048,1]{1,0:T(8,128)} %reshape_reshape.4.marks_ref), custom_call_target="tpu_custom_call" | custom-call | flops 4882169856 | bytes 8716288 | tf_op jit(solution)/shard_map/pallas_call | solution.py:33
  130.0 2.8 %copy.108 = f32[4,16,4,4,8]{4,3,0,1,2:T(4,128)S(1)} copy(f32[4,16,4,4,8]{0,4,3,2,1:T(8,128)} %bitcast.66) | data formatting | bytes 65536 | tf_op jit(solution)/shard_map/transpose | solution.py:89
  132.8 1.2 reshape.231
  134.0 13.3 %all-to-all-start.2 = ((f32[64,1,128]{2,1,0:T(1,128)}), f32[64,1,128]{2,1,0:T(1,128)S(1)}, u32[]{:S(2)}, u32[]{:S(2)}) async-start(f32[64,1,128]{2,1,0:T(1,128)} %reshape.231), calls=%async_computation.2 | async-start | bytes 65536 | tf_op jit(solution)/shard_map/all_to_all | solution.py:122
  147.3 13.3 %all-to-all-done.2 = f32[64,1,128]{2,1,0:T(1,128)S(1)} async-done(((f32[64,1,128]{2,1,0:T(1,128)}), f32[64,1,128]{2,1,0:T(1,128)S(1)}, u32[]{:S(2)}, u32[]{:S(2)}) %all-to-all-start.2) | async-done | bytes 32800 | tf_op jit(solution)/shard_map/all_to_all | solution.py:122
  163.2 1.2 gather_fusion.5
  164.3 6.5 %all-to-all-start.3 = ((f32[8,2,4]{2,1,0:T(2,128)}), f32[8,2,4]{2,1,0:T(2,128)S(1)}, u32[]{:S(2)}, u32[]{:S(2)}) async-start(f32[8,2,4]{2,1,0:T(2,128)} %gather_fusion.5), calls=%async_computation.3 | async-start | bytes 16384 | tf_op jit(solution)/shard_map/all_to_all | solution.py:135
  170.8 4.6 %all-to-all-done.3 = f32[8,2,4]{2,1,0:T(2,128)S(1)} async-done(((f32[8,2,4]{2,1,0:T(2,128)}), f32[8,2,4]{2,1,0:T(2,128)S(1)}, u32[]{:S(2)}, u32[]{:S(2)}) %all-to-all-start.3) | async-done | bytes 288 | tf_op jit(solution)/shard_map/all_to_all | solution.py:135
  (53 shorter events, 8.8 us)
Async XLA Ops:
  7.2 15.3 %copy-start = (s32[64]{0:T(128)S(1)}, s32[64]{0:T(128)}, u32[]{:S(2)}) copy-start(s32[64]{0:T(128)} %param.11) | copy-start | bytes 772
  7.2 52.0 %copy-start.1 = (bf16[776,1536]{1,0:T(8,128)(2,1)S(1)}, bf16[776,1536]{1,0:T(8,128)(2,1)}, u32[]{:S(2)}) copy-start(bf16[776,1536]{1,0:T(8,128)(2,1)} %param.9) | copy-start | bytes 7151620
  7.2 109.9 %all-gather.2.cloned.1.call-start = ((), (), s32[]{:S(2)}) async-start(), calls=%async_computation.4 | async-start | bytes 6684672 | tf_op jit(solution)/shard_map/all_gather | solution.py:74
  26.7 16.7 %all-to-all-start = ((s32[8,1,4]{2,1,0:T(1,128)}), s32[8,1,4]{2,1,0:T(1,128)S(1)}, u32[]{:S(2)}, u32[]{:S(2)}) async-start(s32[8,1,4]{2,1,0:T(1,128)} %bitcast.23), calls=%async_computation | async-start | bytes 8192 | tf_op jit(solution)/shard_map/all_to_all | solution.py:111
  44.7 31.5 %all-to-all-start.1 = ((s32[64,8,4]{1,2,0:T(4,128)}), s32[64,8,4]{1,2,0:T(4,128)S(1)}, u32[]{:S(2)}, u32[]{:S(2)}) async-start(s32[64,8,4]{1,2,0:T(4,128)} %broadcast_in_dim.39), calls=%async_computation.1 | async-start | bytes 262144 | tf_op jit(solution)/shard_map/all_to_all | solution.py:114
  134.0 26.7 %all-to-all-start.2 = ((f32[64,1,128]{2,1,0:T(1,128)}), f32[64,1,128]{2,1,0:T(1,128)S(1)}, u32[]{:S(2)}, u32[]{:S(2)}) async-start(f32[64,1,128]{2,1,0:T(1,128)} %reshape.231), calls=%async_computation.2 | async-start | bytes 65536 | tf_op jit(solution)/shard_map/all_to_all | solution.py:122
  164.3 11.1 %all-to-all-start.3 = ((f32[8,2,4]{2,1,0:T(2,128)}), f32[8,2,4]{2,1,0:T(2,128)S(1)}, u32[]{:S(2)}, u32[]{:S(2)}) async-start(f32[8,2,4]{2,1,0:T(2,128)} %gather_fusion.5), calls=%async_computation.3 | async-start | bytes 16384 | tf_op jit(solution)/shard_map/all_to_all | solution.py:135
Sparse Core Ops, SparseCore 0:
  21.1 95.9 all-gather.1

commit v6 on v5

--- a/solution.py
+++ b/solution.py
@@ -70,8 +70,13 @@
 
     def gather_rows(normed):
         rows = normed
-        for name in tensor_axes:
-            rows = lax.all_gather(rows, name, axis=1, tiled=True)
+        for i, name in enumerate(tensor_axes):
+            if i == 0 and len(tensor_axes) > 1:
+                spread = jnp.broadcast_to(rows[None], (tensor_size[0],) + rows.shape)
+                got = lax.all_to_all(spread, name, split_axis=0, concat_axis=0, tiled=True)
+                rows = jnp.transpose(got, (1, 0, 2, 3)).reshape(rows.shape[0], -1, rows.shape[2])
+            else:
+                rows = lax.all_gather(rows, name, axis=1, tiled=True)
         return rows
 
     def to_gather_order(by_rank):

time: 185 us -> 182 us (0.984)
  starting transfers between devices: 46 us -> 43 us
  waiting for transfers between devices: 70.7 us -> 73.2 us
    all_gather x1 -> x0, blocking collectives: 11.5 us -> none  [gather_rows(): rows = lax.all_gather(rows, name, axis=1, tiled=True)]
    all_to_all x0 -> x1, blocking collectives: none -> 11 us  [gather_rows(): got = lax.all_to_all(spread, name, split_axis=0, concat_axis=0, tiled=True)]
    all_to_all x1, starting transfers between devices: 11.7 us -> 9.48 us  [local(): lax.all_to_all(marked[send_order], 'dp', split_axis=0, concat_axis=0, til...]
    unnamed x9 -> x11, local copies, waits for them, and re-layouts: 6.16 us -> 6.17 us
  transfers between devices with their start and end apart: 5 -> 5, of which waited for: 4 -> 5; matrix products, arithmetic and copies ran while one was open for 9% -> 8% of each run, Pallas kernels for 0% -> 0%
where the time goes in v6:
time: 182 us; the launch traced here: 181 us
  waiting for transfers between devices  73.2 us (40%)
  starting transfers between devices  43 us (24%)
  local copies, waits for them, and re-layouts  18.7 us (10%)
  between operations  14.2 us (8%)
  Pallas kernels  12.8 us (7%)
  blocking collectives  11 us (6%)
  other arithmetic  8.32 us (5%)
    all_gather x1, waiting for transfers between devices, gather_rows(): rows = lax.all_gather(rows, name, axis=1, tiled=True)  41.3 us
    all_to_all x1, starting transfers between devices, local(): lax.all_to_all(spread, tensor_axes, split_axis=0, concat_axis=0, tiled=True)  14.2 us
    all_to_all x1, waiting for transfers between devices, local(): lax.all_to_all(stats, tensor_axes, split_axis=0, concat_axis=0, tiled=True)  13.3 us
    all_to_all x1, waiting for transfers between devices, local(): lax.all_to_all(spread, tensor_axes, split_axis=0, concat_axis=0, tiled=True)  13 us
    pallas_call x1, Pallas kernels, row_stats(): pl.pallas_call(stats_kernel, grid=(n // block,), in_specs=[pl.BlockSpec(m...  12.8 us
    all_to_all x1, starting transfers between devices, local(): lax.all_to_all(stats, tensor_axes, split_axis=0, concat_axis=0, tiled=True)  12.8 us
    all_to_all x1, blocking collectives, gather_rows(): got = lax.all_to_all(spread, name, split_axis=0, concat_axis=0, tiled=True)  11 us
    all_to_all x1, starting transfers between devices, local(): lax.all_to_all(marked[send_order], 'dp', split_axis=0, concat_axis=0, til...  9.48 us
  transfers between devices with their start and end apart: 5, of which 5 were waited for; matrix products, arithmetic and copies ran while one was open for 8% of the time, Pallas kernels for 0%

profile of v6, /device:TPU:1, one launch (start us, length us, event | category | flops | bytes accessed | tf_op | source)
XLA Modules:
  0.0 181.3 jit_solution(5318062824638083071)
XLA Ops:
  7.2 1.2 fusion
  8.4 1.0 fusion.2
  9.5 11.0 %all_to_all.32 = bf16[4,8,4,1536]{3,1,2,0:T(8,128)(2,1)} all-to-all(bf16[4,8,4,1536]{3,1,2,0:T(8,128)(2,1)S(1)} %broadcast_in_dim.45), channel_id=1, replica_groups=mesh['dp'=8,'tx'=4,'tz'=16] {'tx'}, dimensions={0} | all-to-all | bytes 786432 | tf_op jit(solution)/shard_map/all_to_all | solution.py:76
  20.5 0.8 copy.36
  23.4 1.0 sort.65
  24.4 1.1 gather_fusion.2
  25.6 9.5 %all-to-all-start = ((s32[8,1,4]{2,1,0:T(1,128)}), s32[8,1,4]{2,1,0:T(1,128)S(1)}, u32[]{:S(2)}, u32[]{:S(2)}) async-start(s32[8,1,4]{2,1,0:T(1,128)} %bitcast.25), calls=%async_computation | async-start | bytes 8192 | tf_op jit(solution)/shard_map/all_to_all | solution.py:116
  35.1 2.0 %sort.66 = (s32[64]{0:T(128)}, s32[64]{0:T(128)S(1)}) sort(s32[64]{0:T(128)S(1)} %compare_convert_fusion, s32[64]{0:T(128)S(1)} %iota.27), dimensions={0}, to_apply=%region_1.2 | sort | flops 384 | bytes 1024 | tf_op jit(solution)/shard_map/jit(argsort)/sort | solution.py:106
  37.8 1.0 sort.67
  38.8 0.9 all-to-all-done
  41.0 14.2 %all-to-all-start.2 = ((s32[64,8,4]{1,2,0:T(4,128)}), s32[64,8,4]{1,2,0:T(4,128)S(1)}, u32[]{:S(2)}, u32[]{:S(2)}) async-start(s32[64,8,4]{1,2,0:T(4,128)} %broadcast_in_dim.46), calls=%async_computation.2 | async-start | bytes 262144 | tf_op jit(solution)/shard_map/all_to_all | solution.py:119
  55.2 2.8 %copy.43 = bf16[776,1536]{0,1:T(8,128)(2,1)} copy(bf16[776,1536]{1,0:T(8,128)(2,1)S(1)} %copy-done.2) | data formatting | bytes 4767744 | tf_op args[2]
  58.0 1.0 sort.68
  59.0 13.0 %all-to-all-done.2 = s32[64,8,4]{1,2,0:T(4,128)S(1)} async-done(((s32[64,8,4]{1,2,0:T(4,128)}), s32[64,8,4]{1,2,0:T(4,128)S(1)}, u32[]{:S(2)}, u32[]{:S(2)}) %all-to-all-start.2) | async-done | bytes 8224 | tf_op jit(solution)/shard_map/all_to_all | solution.py:119
  72.0 1.3 reshape_reshape.4.marks_ref
  73.4 41.3 %all-gather.2.cloned.1.call-done = bf16[8,256,1536]{2,0,1:T(8,128)(2,1)} async-done(((bf16[8,16,1536]{2,0,1:T(8,128)(2,1)}), bf16[8,256,1536]{2,0,1:T(8,128)(2,1)}) %all-gather.2.cloned.1.call-update) | async-done | bytes 6291472 | tf_op jit(solution)/shard_map/all_gather | solution.py:79
  114.7 12.8 %shard_map.86 = f32[2048,4]{1,0:T(8,128)} custom-call(s32[1]{0:T(128)} %bitcast.3.offset_ref, bf16[2048,1536]{1,0:T(8,128)(2,1)} %bitcast.77, bf16[1536,776]{1,0:T(8,128)(2,1)} %bitcast.64, s32[2048,1]{1,0:T(8,128)} %reshape_reshape.4.marks_ref), custom_call_target="tpu_custom_call" | custom-call | flops 4882169856 | bytes 8716288 | tf_op jit(solution)/shard_map/pallas_call | solution.py:33
  127.6 2.8 %copy.77 = f32[4,16,4,4,8]{4,3,0,1,2:T(4,128)S(1)} copy(f32[4,16,4,4,8]{0,4,3,2,1:T(8,128)} %bitcast.70) | data formatting | bytes 65536 | tf_op jit(solution)/shard_map/transpose | solution.py:94
  130.4 1.2 reshape.236
  131.6 12.8 %all-to-all-start.3 = ((f32[64,1,128]{2,1,0:T(1,128)}), f32[64,1,128]{2,1,0:T(1,128)S(1)}, u32[]{:S(2)}, u32[]{:S(2)}) async-start(f32[64,1,128]{2,1,0:T(1,128)} %reshape.236), calls=%async_computation.3 | async-start | bytes 65536 | tf_op jit(solution)/shard_map/all_to_all | solution.py:127
  144.4 13.3 %all-to-all-done.3 = f32[64,1,128]{2,1,0:T(1,128)S(1)} async-done(((f32[64,1,128]{2,1,0:T(1,128)}), f32[64,1,128]{2,1,0:T(1,128)S(1)}, u32[]{:S(2)}, u32[]{:S(2)}) %all-to-all-start.3) | async-done | bytes 32800 | tf_op jit(solution)/shard_map/all_to_all | solution.py:127
  160.2 1.2 gather_fusion.5
  161.4 6.5 %all-to-all-start.4 = ((f32[8,2,4]{2,1,0:T(2,128)}), f32[8,2,4]{2,1,0:T(2,128)S(1)}, u32[]{:S(2)}, u32[]{:S(2)}) async-start(f32[8,2,4]{2,1,0:T(2,128)} %gather_fusion.5), calls=%async_computation.4 | async-start | bytes 16384 | tf_op jit(solution)/shard_map/all_to_all | solution.py:140
  167.9 4.6 %all-to-all-done.4 = f32[8,2,4]{2,1,0:T(2,128)S(1)} async-done(((f32[8,2,4]{2,1,0:T(2,128)}), f32[8,2,4]{2,1,0:T(2,128)S(1)}, u32[]{:S(2)}, u32[]{:S(2)}) %all-to-all-start.4) | async-done | bytes 288 | tf_op jit(solution)/shard_map/all_to_all | solution.py:140
  (57 shorter events, 8.7 us)
Async XLA Ops:
  7.2 14.9 %copy-start = (s32[64]{0:T(128)S(1)}, s32[64]{0:T(128)}, u32[]{:S(2)}) copy-start(s32[64]{0:T(128)} %param.11) | copy-start | bytes 772
  7.2 15.5 %copy-start.1 = (s32[64]{0:T(128)S(1)}, s32[64]{0:T(128)}, u32[]{:S(2)}) copy-start(s32[64]{0:T(128)} %param.13) | copy-start | bytes 772
  7.2 48.0 %copy-start.2 = (bf16[776,1536]{1,0:T(8,128)(2,1)S(1)}, bf16[776,1536]{1,0:T(8,128)(2,1)}, u32[]{:S(2)}) copy-start(bf16[776,1536]{1,0:T(8,128)(2,1)} %param.9) | copy-start | bytes 7151620
  7.2 107.5 %all-gather.2.cloned.1.call-start = ((), (), s32[]{:S(2)}) async-start(), calls=%async_computation.5 | async-start | bytes 6684672 | tf_op jit(solution)/shard_map/all_gather | solution.py:79
  25.6 14.1 %all-to-all-start = ((s32[8,1,4]{2,1,0:T(1,128)}), s32[8,1,4]{2,1,0:T(1,128)S(1)}, u32[]{:S(2)}, u32[]{:S(2)}) async-start(s32[8,1,4]{2,1,0:T(1,128)} %bitcast.25), calls=%async_computation | async-start | bytes 8192 | tf_op jit(solution)/shard_map/all_to_all | solution.py:116
  41.0 31.0 %all-to-all-start.2 = ((s32[64,8,4]{1,2,0:T(4,128)}), s32[64,8,4]{1,2,0:T(4,128)S(1)}, u32[]{:S(2)}, u32[]{:S(2)}) async-start(s32[64,8,4]{1,2,0:T(4,128)} %broadcast_in_dim.46), calls=%async_computation.2 | async-start | bytes 262144 | tf_op jit(solution)/shard_map/all_to_all | solution.py:119
  131.6 26.1 %all-to-all-start.3 = ((f32[64,1,128]{2,1,0:T(1,128)}), f32[64,1,128]{2,1,0:T(1,128)S(1)}, u32[]{:S(2)}, u32[]{:S(2)}) async-start(f32[64,1,128]{2,1,0:T(1,128)} %reshape.236), calls=%async_computation.3 | async-start | bytes 65536 | tf_op jit(solution)/shard_map/all_to_all | solution.py:127
  161.4 11.1 %all-to-all-start.4 = ((f32[8,2,4]{2,1,0:T(2,128)}), f32[8,2,4]{2,1,0:T(2,128)S(1)}, u32[]{:S(2)}, u32[]{:S(2)}) async-start(f32[8,2,4]{2,1,0:T(2,128)} %gather_fusion.5), calls=%async_computation.4 | async-start | bytes 16384 | tf_op jit(solution)/shard_map/all_to_all | solution.py:140
Sparse Core Ops, SparseCore 0:
  20.6 94.0 all-gather.1

commit v7 on v6

--- a/solution.py
+++ b/solution.py
@@ -62,7 +62,7 @@
     return slow, row.size // slow
 
 
-def local_fn(tensor_axes, tensor_size):
+def local_fn(tensor_axes, tensor_size, dp_size):
     def tensor_rank():
         if len(tensor_axes) == 1:
             return lax.axis_index(tensor_axes[0])
@@ -93,6 +93,20 @@
         grid = stats.reshape(k, tensor_size[1], tensor_size[0], w, s)
         grid = jnp.transpose(grid, (2, 1, 0, 4, 3))
         return grid.reshape(tensor_size[0] * tensor_size[1], k, s, w)
+
+    def exchange(chunks, group_rank):
+        groups = chunks.shape[0] // (chunks.shape[0] // dp_size)
+        per = chunks.shape[0] // groups
+        blocks = chunks.reshape((groups, per) + chunks.shape[1:])
+        got = []
+        for shift in range(groups):
+            send = jnp.take(blocks, (group_rank + shift) % groups, axis=0)
+            if shift:
+                send = lax.ppermute(send, "dp", [(i, (i + shift) % groups) for i in range(groups)])
+            got.append(send)
+        order = (group_rank - jnp.arange(groups)) % groups
+        by_source = jnp.stack(got)[jnp.argsort(order)]
+        return by_source.reshape(chunks.shape)
 
     def local(hidden, norm_gain, embedding, targets, lengths, loss_mask, deal_slots):
         group_rank = lax.axis_index("dp")
@@ -137,7 +151,7 @@
         entropy = jnp.where(usable_rows, log_total - weighted / totals, 0.0)
 
         both = jnp.stack([log_prob, entropy], axis=1)[arrived_slot]
-        returned = lax.all_to_all(both, "dp", split_axis=0, concat_axis=0, tiled=True)[undo_order]
+        returned = exchange(both, group_rank)[undo_order]
         return returned[:, 0], returned[:, 1]
 
     return local
@@ -162,7 +176,7 @@
         P(),
     )
     return jax.shard_map(
-        local_fn(tensor_axes, tensor_size),
+        local_fn(tensor_axes, tensor_size, mesh.shape["dp"]),
         mesh=run_mesh,
         in_specs=placed,
         out_specs=(P("dp", tensor), P("dp", tensor)),

time: 182 us -> 193 us (1.060)
  starting transfers between devices: 43 us -> 57.2 us
  waiting for transfers between devices: 73.2 us -> 69.5 us
    ppermute x0 -> x7, starting transfers between devices: none -> 20.4 us  [exchange(): lax.ppermute(send, 'dp', [(i, (i + shift) % groups) for i in range(groups)])]
    all_to_all x1 -> x0, starting transfers between devices: 6.52 us -> none  [local(): lax.all_to_all(both, 'dp', split_axis=0, concat_axis=0, tiled=True)]
    all_to_all x1 -> x0, waiting for transfers between devices: 4.61 us -> none  [local(): lax.all_to_all(both, 'dp', split_axis=0, concat_axis=0, tiled=True)]
    unnamed x11 -> x22, local copies, waits for them, and re-layouts: 6.17 us -> 4.88 us
  transfers between devices with their start and end apart: 5 -> 11, of which waited for: 5 -> 5; matrix products, arithmetic and copies ran while one was open for 8% -> 8% of each run, Pallas kernels for 0% -> 0%
where the time goes in v7:
time: 193 us
  waiting for transfers between devices  69.5 us (36%)
  starting transfers between devices  57.2 us (30%)
  local copies, waits for them, and re-layouts  18.1 us (9%)
  between operations  14.5 us (8%)
  Pallas kernels  12.8 us (7%)
  blocking collectives  11 us (6%)
  other arithmetic  9.48 us (5%)
    all_gather x1, waiting for transfers between devices, gather_rows(): rows = lax.all_gather(rows, name, axis=1, tiled=True)  39.8 us
    ppermute x7, starting transfers between devices, exchange(): lax.ppermute(send, 'dp', [(i, (i + shift) % groups) for i in range(groups)])  20.4 us
    all_to_all x1, starting transfers between devices, local(): lax.all_to_all(spread, tensor_axes, split_axis=0, concat_axis=0, tiled=True)  14.2 us
    all_to_all x1, waiting for transfers between devices, local(): lax.all_to_all(spread, tensor_axes, split_axis=0, concat_axis=0, tiled=True)  13.9 us
    all_to_all x1, waiting for transfers between devices, local(): lax.all_to_all(stats, tensor_axes, split_axis=0, concat_axis=0, tiled=True)  13.2 us
    all_to_all x1, starting transfers between devices, local(): lax.all_to_all(stats, tensor_axes, split_axis=0, concat_axis=0, tiled=True)  13 us
    pallas_call x1, Pallas kernels, row_stats(): pl.pallas_call(stats_kernel, grid=(n // block,), in_specs=[pl.BlockSpec(m...  12.8 us
    all_to_all x1, blocking collectives, gather_rows(): got = lax.all_to_all(spread, name, split_axis=0, concat_axis=0, tiled=True)  11 us
  transfers between devices with their start and end apart: 11, of which 5 were waited for; matrix products, arithmetic and copies ran while one was open for 8% of the time, Pallas kernels for 0%

profile of v7, /device:TPU:1, one launch (start us, length us, event | category | flops | bytes accessed | tf_op | source)
XLA Modules:
  0.0 192.6 jit_solution(8734629642958444797)
XLA Ops:
  7.3 1.2 fusion
  9.5 11.0 %all_to_all.27 = bf16[4,8,4,1536]{3,1,2,0:T(8,128)(2,1)} all-to-all(bf16[4,8,4,1536]{3,1,2,0:T(8,128)(2,1)S(1)} %broadcast_in_dim.54), channel_id=1, replica_groups=mesh['dp'=8,'tx'=4,'tz'=16] {'tx'}, dimensions={0} | all-to-all | bytes 786432 | tf_op jit(solution)/shard_map/all_to_all | solution.py:76
  20.6 1.3 gather_fusion.1
  23.7 2.0 %sort.80 = (s32[64]{0:T(128)}, s32[64]{0:T(128)S(1)}) sort(s32[64]{0:T(128)S(1)} %compare_convert_fusion, s32[64]{0:T(128)S(1)} %iota.33), dimensions={0}, to_apply=%region_1.2 | sort | flops 384 | bytes 1024 | tf_op jit(solution)/shard_map/jit(argsort)/sort | solution.py:120
  25.8 1.1 gather_fusion.2
  27.0 9.5 %all-to-all-start = ((s32[8,1,4]{2,1,0:T(1,128)}), s32[8,1,4]{2,1,0:T(1,128)S(1)}, u32[]{:S(2)}, u32[]{:S(2)}) async-start(s32[8,1,4]{2,1,0:T(1,128)} %bitcast.34), calls=%async_computation | async-start | bytes 8192 | tf_op jit(solution)/shard_map/all_to_all | solution.py:130
  42.4 14.2 %all-to-all-start.2 = ((s32[64,8,4]{1,2,0:T(4,128)}), s32[64,8,4]{1,2,0:T(4,128)S(1)}, u32[]{:S(2)}, u32[]{:S(2)}) async-start(s32[64,8,4]{1,2,0:T(4,128)} %broadcast_in_dim.55), calls=%async_computation.2 | async-start | bytes 262144 | tf_op jit(solution)/shard_map/all_to_all | solution.py:133
  56.6 2.8 %copy.47 = bf16[776,1536]{0,1:T(8,128)(2,1)} copy(bf16[776,1536]{1,0:T(8,128)(2,1)S(1)} %copy-done.2) | data formatting | bytes 4767744 | tf_op args[2]
  59.4 13.9 %all-to-all-done.2 = s32[64,8,4]{1,2,0:T(4,128)S(1)} async-done(((s32[64,8,4]{1,2,0:T(4,128)}), s32[64,8,4]{1,2,0:T(4,128)S(1)}, u32[]{:S(2)}, u32[]{:S(2)}) %all-to-all-start.2) | async-done | bytes 8224 | tf_op jit(solution)/shard_map/all_to_all | solution.py:133
  73.4 1.3 reshape_reshape.4.marks_ref
  74.7 39.8 %all-gather.2.cloned.1.call-done = bf16[8,256,1536]{2,0,1:T(8,128)(2,1)} async-done(((bf16[8,16,1536]{2,0,1:T(8,128)(2,1)}), bf16[8,256,1536]{2,0,1:T(8,128)(2,1)}) %all-gather.2.cloned.1.call-update) | async-done | bytes 6291472 | tf_op jit(solution)/shard_map/all_gather | solution.py:79
  114.5 12.8 %shard_map.86 = f32[2048,4]{1,0:T(8,128)} custom-call(s32[1]{0:T(128)} %bitcast.3.offset_ref, bf16[2048,1536]{1,0:T(8,128)(2,1)} %bitcast.111, bf16[1536,776]{1,0:T(8,128)(2,1)} %bitcast.89, s32[2048,1]{1,0:T(8,128)} %reshape_reshape.4.marks_ref), custom_call_target="tpu_custom_call" | custom-call | flops 4882169856 | bytes 8716288 | tf_op jit(solution)/shard_map/pallas_call | solution.py:33
  127.3 2.8 %copy.85 = f32[4,16,4,4,8]{4,3,0,1,2:T(4,128)S(1)} copy(f32[4,16,4,4,8]{0,4,3,2,1:T(8,128)} %bitcast.95) | data formatting | bytes 65536 | tf_op jit(solution)/shard_map/transpose | solution.py:94
  130.2 1.2 reshape.407
  131.3 13.0 %all-to-all-start.3 = ((f32[64,1,128]{2,1,0:T(1,128)}), f32[64,1,128]{2,1,0:T(1,128)S(1)}, u32[]{:S(2)}, u32[]{:S(2)}) async-start(f32[64,1,128]{2,1,0:T(1,128)} %reshape.407), calls=%async_computation.3 | async-start | bytes 65536 | tf_op jit(solution)/shard_map/all_to_all | solution.py:141
  144.6 13.2 %all-to-all-done.3 = f32[64,1,128]{2,1,0:T(1,128)S(1)} async-done(((f32[64,1,128]{2,1,0:T(1,128)}), f32[64,1,128]{2,1,0:T(1,128)S(1)}, u32[]{:S(2)}, u32[]{:S(2)}) %all-to-all-start.3) | async-done | bytes 32800 | tf_op jit(solution)/shard_map/all_to_all | solution.py:141
  161.1 3.3 %collective-permute-start = (f32[1,2,4]{2,1,0:T(2,128)S(1)}, f32[1,2,4]{2,1,0:T(2,128)S(1)}, u32[]{:S(2)}, u32[]{:S(2)}) collective-permute-start(f32[1,2,4]{2,1,0:T(2,128)S(1)} %bitcast.110), channel_id=1, source_target_pairs={{0,64},{64,128},{128,192},{192,256},{256,320},{320,384},{384,448},... | collective-permute-start | bytes 104 | tf_op jit(solution)/shard_map/ppermute | solution.py:105
  164.4 3.1 %collective-permute-start.1 = (f32[1,2,4]{2,1,0:T(2,128)S(1)}, f32[1,2,4]{2,1,0:T(2,128)S(1)}, u32[]{:S(2)}, u32[]{:S(2)}) collective-permute-start(f32[1,2,4]{2,1,0:T(2,128)S(1)} %bitcast.109), channel_id=1, source_target_pairs={{0,128},{64,192},{128,256},{192,320},{256,384},{320,448},{384,0},{... | collective-permute-start | bytes 104 | tf_op jit(solution)/shard_map/ppermute | solution.py:105
  167.6 3.5 %collective-permute-start.2 = (f32[1,2,4]{2,1,0:T(2,128)S(1)}, f32[1,2,4]{2,1,0:T(2,128)S(1)}, u32[]{:S(2)}, u32[]{:S(2)}) collective-permute-start(f32[1,2,4]{2,1,0:T(2,128)S(1)} %bitcast.108), channel_id=1, source_target_pairs={{0,192},{64,256},{128,320},{192,384},{256,448},{320,0},{384,64},{4... | collective-permute-start | bytes 104 | tf_op jit(solution)/shard_map/ppermute | solution.py:105
  171.0 2.4 %collective-permute-start.3 = (f32[1,2,4]{2,1,0:T(2,128)S(1)}, f32[1,2,4]{2,1,0:T(2,128)S(1)}, u32[]{:S(2)}, u32[]{:S(2)}) collective-permute-start(f32[1,2,4]{2,1,0:T(2,128)S(1)} %bitcast.107), channel_id=1, source_target_pairs={{0,256},{64,320},{128,384},{192,448},{256,0},{320,64},{384,128},{4... | collective-permute-start | bytes 104 | tf_op jit(solution)/shard_map/ppermute | solution.py:105
  173.5 3.9 %collective-permute-start.4 = (f32[1,2,4]{2,1,0:T(2,128)S(1)}, f32[1,2,4]{2,1,0:T(2,128)S(1)}, u32[]{:S(2)}, u32[]{:S(2)}) collective-permute-start(f32[1,2,4]{2,1,0:T(2,128)S(1)} %bitcast.106), channel_id=1, source_target_pairs={{0,320},{64,384},{128,448},{192,0},{256,64},{320,128},{384,192},{4... | collective-permute-start | bytes 104 | tf_op jit(solution)/shard_map/ppermute | solution.py:105
  177.4 2.6 %collective-permute-start.5 = (f32[1,2,4]{2,1,0:T(2,128)S(1)}, f32[1,2,4]{2,1,0:T(2,128)S(1)}, u32[]{:S(2)}, u32[]{:S(2)}) collective-permute-start(f32[1,2,4]{2,1,0:T(2,128)S(1)} %bitcast.105), channel_id=1, source_target_pairs={{0,384},{64,448},{128,0},{192,64},{256,128},{320,192},{384,256},{4... | collective-permute-start | bytes 104 | tf_op jit(solution)/shard_map/ppermute | solution.py:105
  180.0 1.6 collective-permute-start.6
  181.7 1.6 collective-permute-done.6
  (88 shorter events, 14.9 us)
Async XLA Ops:
  7.2 14.7 %copy-start = (s32[64]{0:T(128)S(1)}, s32[64]{0:T(128)}, u32[]{:S(2)}) copy-start(s32[64]{0:T(128)} %param.13) | copy-start | bytes 772
  7.2 16.5 %copy-start.1 = (s32[64]{0:T(128)S(1)}, s32[64]{0:T(128)}, u32[]{:S(2)}) copy-start(s32[64]{0:T(128)} %param.15) | copy-start | bytes 772
  7.2 15.3 %copy-start.3 = (s32[8,4]{0,1:T(4,128)S(1)}, s32[8,4]{0,1:T(4,128)}, u32[]{:S(2)}) copy-start(s32[8,4]{0,1:T(4,128)} %param.14) | copy-start | bytes 388
  7.2 15.4 %copy-start.4 = (s32[8,4]{0,1:T(4,128)S(1)}, s32[8,4]{0,1:T(4,128)}, u32[]{:S(2)}) copy-start(s32[8,4]{0,1:T(4,128)} %param.12) | copy-start | bytes 388
  7.2 49.4 %copy-start.2 = (bf16[776,1536]{1,0:T(8,128)(2,1)S(1)}, bf16[776,1536]{1,0:T(8,128)(2,1)}, u32[]{:S(2)}) copy-start(bf16[776,1536]{1,0:T(8,128)(2,1)} %param.11) | copy-start | bytes 7151620
  7.2 107.3 %all-gather.2.cloned.1.call-start = ((), (), s32[]{:S(2)}) async-start(), calls=%async_computation.4 | async-start | bytes 6684672 | tf_op jit(solution)/shard_map/all_gather | solution.py:79
  27.0 14.1 %all-to-all-start = ((s32[8,1,4]{2,1,0:T(1,128)}), s32[8,1,4]{2,1,0:T(1,128)S(1)}, u32[]{:S(2)}, u32[]{:S(2)}) async-start(s32[8,1,4]{2,1,0:T(1,128)} %bitcast.34), calls=%async_computation | async-start | bytes 8192 | tf_op jit(solution)/shard_map/all_to_all | solution.py:130
  42.4 31.0 %all-to-all-start.2 = ((s32[64,8,4]{1,2,0:T(4,128)}), s32[64,8,4]{1,2,0:T(4,128)S(1)}, u32[]{:S(2)}, u32[]{:S(2)}) async-start(s32[64,8,4]{1,2,0:T(4,128)} %broadcast_in_dim.55), calls=%async_computation.2 | async-start | bytes 262144 | tf_op jit(solution)/shard_map/all_to_all | solution.py:133
  131.3 26.4 %all-to-all-start.3 = ((f32[64,1,128]{2,1,0:T(1,128)}), f32[64,1,128]{2,1,0:T(1,128)S(1)}, u32[]{:S(2)}, u32[]{:S(2)}) async-start(f32[64,1,128]{2,1,0:T(1,128)} %reshape.407), calls=%async_computation.3 | async-start | bytes 65536 | tf_op jit(solution)/shard_map/all_to_all | solution.py:141
  161.1 16.3 %collective-permute-start = (f32[1,2,4]{2,1,0:T(2,128)S(1)}, f32[1,2,4]{2,1,0:T(2,128)S(1)}, u32[]{:S(2)}, u32[]{:S(2)}) collective-permute-start(f32[1,2,4]{2,1,0:T(2,128)S(1)} %bitcast.110), channel_id=1, source_target_pairs={{0,64},{64,128},{128,192},{192,256},{256,320},{320,384},{384,448},... | collective-permute-start | bytes 104 | tf_op jit(solution)/shard_map/ppermute | solution.py:105
  164.4 15.5 %collective-permute-start.1 = (f32[1,2,4]{2,1,0:T(2,128)S(1)}, f32[1,2,4]{2,1,0:T(2,128)S(1)}, u32[]{:S(2)}, u32[]{:S(2)}) collective-permute-start(f32[1,2,4]{2,1,0:T(2,128)S(1)} %bitcast.109), channel_id=1, source_target_pairs={{0,128},{64,192},{128,256},{192,320},{256,384},{320,448},{384,0},{... | collective-permute-start | bytes 104 | tf_op jit(solution)/shard_map/ppermute | solution.py:105
  167.6 14.1 %collective-permute-start.2 = (f32[1,2,4]{2,1,0:T(2,128)S(1)}, f32[1,2,4]{2,1,0:T(2,128)S(1)}, u32[]{:S(2)}, u32[]{:S(2)}) collective-permute-start(f32[1,2,4]{2,1,0:T(2,128)S(1)} %bitcast.108), channel_id=1, source_target_pairs={{0,192},{64,256},{128,320},{192,384},{256,448},{320,0},{384,64},{4... | collective-permute-start | bytes 104 | tf_op jit(solution)/shard_map/ppermute | solution.py:105
  171.0 10.6 %collective-permute-start.3 = (f32[1,2,4]{2,1,0:T(2,128)S(1)}, f32[1,2,4]{2,1,0:T(2,128)S(1)}, u32[]{:S(2)}, u32[]{:S(2)}) collective-permute-start(f32[1,2,4]{2,1,0:T(2,128)S(1)} %bitcast.107), channel_id=1, source_target_pairs={{0,256},{64,320},{128,384},{192,448},{256,0},{320,64},{384,128},{4... | collective-permute-start | bytes 104 | tf_op jit(solution)/shard_map/ppermute | solution.py:105
  173.5 8.2 %collective-permute-start.4 = (f32[1,2,4]{2,1,0:T(2,128)S(1)}, f32[1,2,4]{2,1,0:T(2,128)S(1)}, u32[]{:S(2)}, u32[]{:S(2)}) collective-permute-start(f32[1,2,4]{2,1,0:T(2,128)S(1)} %bitcast.106), channel_id=1, source_target_pairs={{0,320},{64,384},{128,448},{192,0},{256,64},{320,128},{384,192},{4... | collective-permute-start | bytes 104 | tf_op jit(solution)/shard_map/ppermute | solution.py:105
  177.4 4.3 %collective-permute-start.5 = (f32[1,2,4]{2,1,0:T(2,128)S(1)}, f32[1,2,4]{2,1,0:T(2,128)S(1)}, u32[]{:S(2)}, u32[]{:S(2)}) collective-permute-start(f32[1,2,4]{2,1,0:T(2,128)S(1)} %bitcast.105), channel_id=1, source_target_pairs={{0,384},{64,448},{128,0},{192,64},{256,128},{320,192},{384,256},{4... | collective-permute-start | bytes 104 | tf_op jit(solution)/shard_map/ppermute | solution.py:105
  180.0 3.3 %collective-permute-start.6 = (f32[1,2,4]{2,1,0:T(2,128)S(1)}, f32[1,2,4]{2,1,0:T(2,128)S(1)}, u32[]{:S(2)}, u32[]{:S(2)}) collective-permute-start(f32[1,2,4]{2,1,0:T(2,128)S(1)} %bitcast.104), channel_id=1, source_target_pairs={{0,448},{64,0},{128,64},{192,128},{256,192},{320,256},{384,320},{4... | collective-permute-start | bytes 104 | tf_op jit(solution)/shard_map/ppermute | solution.py:105
Sparse Core Ops, SparseCore 0:
  20.7 93.7 all-gather.1

commit v8 on v6

--- a/solution.py
+++ b/solution.py
@@ -12,40 +12,42 @@
 ROW_BLOCK = 512
 
 
-def stats_kernel(offset_ref, rows_ref, emb_ref, marks_ref, out_ref):
-    logits = jnp.dot(rows_ref[...], emb_ref[...], preferred_element_type=jnp.float32)
-    columns = offset_ref[0] + lax.broadcasted_iota(jnp.int32, (1, logits.shape[1]), 1)
+def stats_kernel(offset_ref, emb_ref, rows_ref, marks_ref, out_ref):
+    logits = lax.dot_general(
+        emb_ref[...], rows_ref[...], (((1,), (1,)), ((), ())), preferred_element_type=jnp.float32
+    )
+    columns = offset_ref[0] + lax.broadcasted_iota(jnp.int32, (logits.shape[0], 1), 0)
     bias = jnp.where(columns < VREAL, 0.0, -jnp.inf)
     masked = logits + bias
-    maximum = jnp.max(masked, axis=1, keepdims=True)
+    maximum = jnp.max(masked, axis=0, keepdims=True)
     shift = jnp.maximum(maximum, jnp.finfo(jnp.float32).min)
     weights = jnp.exp(masked - shift)
-    totals = jnp.sum(weights, axis=1, keepdims=True)
-    weighted = jnp.sum(weights * logits, axis=1, keepdims=True)
-    chosen = jnp.sum(jnp.where(columns == marks_ref[...], logits, 0.0), axis=1, keepdims=True)
-    out_ref[...] = jnp.concatenate([maximum, totals, weighted, chosen], axis=1)
+    totals = jnp.sum(weights, axis=0, keepdims=True)
+    weighted = jnp.sum(weights * logits, axis=0, keepdims=True)
+    chosen = jnp.sum(jnp.where(columns == marks_ref[...], logits, 0.0), axis=0, keepdims=True)
+    out_ref[...] = jnp.concatenate([maximum, totals, weighted, chosen], axis=0)
 
 
-def row_stats(rows, emb_t, marks, offset):
+def row_stats(rows, embedding, marks, offset):
     n, d = rows.shape
-    v = emb_t.shape[1]
+    v = embedding.shape[0]
     block = ROW_BLOCK if n % ROW_BLOCK == 0 else n
     return pl.pallas_call(
         stats_kernel,
         grid=(n // block,),
         in_specs=[
             pl.BlockSpec(memory_space=pltpu.SMEM),
+            pl.BlockSpec((v, d), lambda i: (0, 0)),
             pl.BlockSpec((block, d), lambda i: (i, 0)),
-            pl.BlockSpec((d, v), lambda i: (0, 0)),
-            pl.BlockSpec((block, 1), lambda i: (i, 0)),
+            pl.BlockSpec((1, block), lambda i: (0, i)),
         ],
-        out_specs=pl.BlockSpec((block, 4), lambda i: (i, 0)),
-        out_shape=jax.ShapeDtypeStruct((n, 4), jnp.float32),
+        out_specs=pl.BlockSpec((4, block), lambda i: (0, i)),
+        out_shape=jax.ShapeDtypeStruct((4, n), jnp.float32),
         cost_estimate=pl.CostEstimate(
             flops=2 * n * v * d, transcendentals=n * v, bytes_accessed=2 * (n + v) * d + 20 * n
         ),
         interpret=INTERPRET,
-    )(offset.reshape(1), rows, emb_t, marks.reshape(n, 1))
+    )(offset.reshape(1), embedding, rows, marks.reshape(1, n))
 
 
 def normalize(hidden, norm_gain):
@@ -121,9 +123,9 @@
 
         offset = (t_rank * embedding.shape[0]).astype(jnp.int32)
         flat_rows = jnp.transpose(row_block, (1, 0, 2)).reshape(-1, row_block.shape[2])
-        local_stats = row_stats(flat_rows, jnp.transpose(embedding), block_marks, offset)
+        local_stats = row_stats(flat_rows, embedding, block_marks, offset)
 
-        stats = from_gather_order(jnp.transpose(local_stats), sequences, row_width)
+        stats = from_gather_order(local_stats, sequences, row_width)
         parts = lax.all_to_all(stats, tensor_axes, split_axis=0, concat_axis=0, tiled=True)
         part_max, part_tot, part_wt, part_ch = parts[:, 0], parts[:, 1], parts[:, 2], parts[:, 3]
         overall = jnp.max(part_max, axis=0)

time: 182 us -> 178 us (0.978)
  local copies, waits for them, and re-layouts: 18.7 us -> 15.2 us
  Pallas kernels: 12.8 us -> 10.8 us
    all_to_all x1, waiting for transfers between devices: 13 us -> 16.1 us  [local(): lax.all_to_all(spread, tensor_axes, split_axis=0, concat_axis=0, tiled=True)]
    unnamed x11 -> x6, local copies, waits for them, and re-layouts: 6.17 us -> 3.3 us
    transpose x1 -> x0, local copies, waits for them, and re-layouts: 2.83 us -> none  [from_gather_order(): grid = jnp.transpose(grid, (2, 1, 0, 4, 3))]
    pallas_call x1, Pallas kernels: 12.8 us -> 10.8 us  [row_stats(): pl.pallas_call(stats_kernel, grid=(n // block,), in_specs=[pl.BlockSpec(m...]
  transfers between devices with their start and end apart: 5 -> 5, of which waited for: 5 -> 4; matrix products, arithmetic and copies ran while one was open for 8% -> 8% of each run, Pallas kernels for 0% -> 0%
where the time goes in v8:
time: 178 us
  waiting for transfers between devices  74.2 us (42%)
  starting transfers between devices  43.5 us (24%)
  local copies, waits for them, and re-layouts  15.2 us (9%)
  between operations  14.2 us (8%)
  blocking collectives  11 us (6%)
  Pallas kernels  10.8 us (6%)
  other arithmetic  8.82 us (5%)
    all_gather x1, waiting for transfers between devices, gather_rows(): rows = lax.all_gather(rows, name, axis=1, tiled=True)  40.2 us
    all_to_all x1, waiting for transfers between devices, local(): lax.all_to_all(spread, tensor_axes, split_axis=0, concat_axis=0, tiled=True)  16.1 us
    all_to_all x1, starting transfers between devices, local(): lax.all_to_all(spread, tensor_axes, split_axis=0, concat_axis=0, tiled=True)  14.1 us
    all_to_all x1, waiting for transfers between devices, local(): lax.all_to_all(stats, tensor_axes, split_axis=0, concat_axis=0, tiled=True)  13.3 us
    all_to_all x1, starting transfers between devices, local(): lax.all_to_all(stats, tensor_axes, split_axis=0, concat_axis=0, tiled=True)  13.2 us
    all_to_all x1, blocking collectives, gather_rows(): got = lax.all_to_all(spread, name, split_axis=0, concat_axis=0, tiled=True)  11 us
    pallas_call x1, Pallas kernels, row_stats(): pl.pallas_call(stats_kernel, grid=(n // block,), in_specs=[pl.BlockSpec(m...  10.8 us
    all_to_all x1, starting transfers between devices, local(): lax.all_to_all(marked[send_order], 'dp', split_axis=0, concat_axis=0, til...  9.55 us
  transfers between devices with their start and end apart: 5, of which 4 were waited for; matrix products, arithmetic and copies ran while one was open for 8% of the time, Pallas kernels for 0%

profile of v8, /device:TPU:1, one launch (start us, length us, event | category | flops | bytes accessed | tf_op | source)
XLA Modules:
  0.0 177.7 jit_solution(8225177544375142182)
XLA Ops:
  7.2 1.0 fusion
  8.3 1.0 fusion.2
  9.3 11.0 %all_to_all.32 = bf16[4,8,4,1536]{3,1,2,0:T(8,128)(2,1)} all-to-all(bf16[4,8,4,1536]{3,1,2,0:T(8,128)(2,1)S(1)} %broadcast_in_dim.45), channel_id=1, replica_groups=mesh['dp'=8,'tx'=4,'tz'=16] {'tx'}, dimensions={0} | all-to-all | bytes 786432 | tf_op jit(solution)/shard_map/all_to_all | solution.py:78
  20.3 0.8 copy.34
  22.5 1.3 gather_fusion.1
  23.9 1.0 sort.65
  24.9 1.1 gather_fusion.2
  26.0 9.5 %all-to-all-start = ((s32[8,1,4]{2,1,0:T(1,128)}), s32[8,1,4]{2,1,0:T(1,128)S(1)}, u32[]{:S(2)}, u32[]{:S(2)}) async-start(s32[8,1,4]{2,1,0:T(1,128)} %bitcast.22), calls=%async_computation | async-start | bytes 8192 | tf_op jit(solution)/shard_map/all_to_all | solution.py:118
  36.3 2.0 %sort.66 = (s32[64]{0:T(128)}, s32[64]{0:T(128)S(1)}) sort(s32[64]{0:T(128)S(1)} %compare_convert_fusion, s32[64]{0:T(128)S(1)} %iota.27), dimensions={0}, to_apply=%region_1.2 | sort | flops 384 | bytes 1024 | tf_op jit(solution)/shard_map/jit(argsort)/sort | solution.py:108
  38.3 1.3 gather_fusion.3
  39.6 1.0 sort.67
  41.9 14.1 %all-to-all-start.2 = ((s32[64,8,4]{1,2,0:T(4,128)}), s32[64,8,4]{1,2,0:T(4,128)S(1)}, u32[]{:S(2)}, u32[]{:S(2)}) async-start(s32[64,8,4]{1,2,0:T(4,128)} %broadcast_in_dim.46), calls=%async_computation.2 | async-start | bytes 262144 | tf_op jit(solution)/shard_map/all_to_all | solution.py:121
  56.1 1.0 sort.68
  57.1 16.1 %all-to-all-done.2 = s32[64,8,4]{1,2,0:T(4,128)S(1)} async-done(((s32[64,8,4]{1,2,0:T(4,128)}), s32[64,8,4]{1,2,0:T(4,128)S(1)}, u32[]{:S(2)}, u32[]{:S(2)}) %all-to-all-start.2) | async-done | bytes 8224 | tf_op jit(solution)/shard_map/all_to_all | solution.py:121
  73.2 0.8 reshape_reshape.3.marks_ref
  73.9 40.2 %all-gather.2.cloned.1.call-done = bf16[8,256,1536]{2,0,1:T(8,128)(2,1)} async-done(((bf16[8,16,1536]{2,0,1:T(8,128)(2,1)}), bf16[8,256,1536]{2,0,1:T(8,128)(2,1)}) %all-gather.2.cloned.1.call-update) | async-done | bytes 6291472 | tf_op jit(solution)/shard_map/all_gather | solution.py:81
  114.1 10.8 %shard_map.86 = f32[4,2048]{1,0:T(4,128)} custom-call(s32[1]{0:T(128)} %bitcast.3.offset_ref, bf16[776,1536]{1,0:T(8,128)(2,1)} %emb_ref.1, bf16[2048,1536]{1,0:T(8,128)(2,1)} %bitcast.70, s32[1,2048]{1,0:T(1,128)} %reshape_reshape.3.marks_ref), custom_call_target="tpu_custom_call" | custom-call | flops 4882169856 | bytes 8716288 | tf_op jit(solution)/shard_map/pallas_call | solution.py:35
  124.9 1.4 reshape.174
  126.4 1.1 reshape.236
  127.6 13.2 %all-to-all-start.3 = ((f32[64,1,128]{2,1,0:T(1,128)}), f32[64,1,128]{2,1,0:T(1,128)S(1)}, u32[]{:S(2)}, u32[]{:S(2)}) async-start(f32[64,1,128]{2,1,0:T(1,128)} %reshape.236), calls=%async_computation.3 | async-start | bytes 65536 | tf_op jit(solution)/shard_map/all_to_all | solution.py:129
  140.8 13.3 %all-to-all-done.3 = f32[64,1,128]{2,1,0:T(1,128)S(1)} async-done(((f32[64,1,128]{2,1,0:T(1,128)}), f32[64,1,128]{2,1,0:T(1,128)S(1)}, u32[]{:S(2)}, u32[]{:S(2)}) %all-to-all-start.3) | async-done | bytes 32800 | tf_op jit(solution)/shard_map/all_to_all | solution.py:129
  156.7 1.2 gather_fusion.5
  157.8 6.5 %all-to-all-start.4 = ((f32[8,2,4]{2,1,0:T(2,128)}), f32[8,2,4]{2,1,0:T(2,128)S(1)}, u32[]{:S(2)}, u32[]{:S(2)}) async-start(f32[8,2,4]{2,1,0:T(2,128)} %gather_fusion.5), calls=%async_computation.4 | async-start | bytes 16384 | tf_op jit(solution)/shard_map/all_to_all | solution.py:142
  164.4 4.6 %all-to-all-done.4 = f32[8,2,4]{2,1,0:T(2,128)S(1)} async-done(((f32[8,2,4]{2,1,0:T(2,128)}), f32[8,2,4]{2,1,0:T(2,128)S(1)}, u32[]{:S(2)}, u32[]{:S(2)}) %all-to-all-start.4) | async-done | bytes 288 | tf_op jit(solution)/shard_map/all_to_all | solution.py:142
  (53 shorter events, 8.2 us)
Async XLA Ops:
  7.2 14.7 %copy-start = (s32[64]{0:T(128)S(1)}, s32[64]{0:T(128)}, u32[]{:S(2)}) copy-start(s32[64]{0:T(128)} %param.11) | copy-start | bytes 772
  7.2 106.9 %all-gather.2.cloned.1.call-start = ((), (), s32[]{:S(2)}) async-start(), calls=%async_computation.5 | async-start | bytes 6684672 | tf_op jit(solution)/shard_map/all_gather | solution.py:81
  26.0 14.6 %all-to-all-start = ((s32[8,1,4]{2,1,0:T(1,128)}), s32[8,1,4]{2,1,0:T(1,128)S(1)}, u32[]{:S(2)}, u32[]{:S(2)}) async-start(s32[8,1,4]{2,1,0:T(1,128)} %bitcast.22), calls=%async_computation | async-start | bytes 8192 | tf_op jit(solution)/shard_map/all_to_all | solution.py:118
  41.9 31.2 %all-to-all-start.2 = ((s32[64,8,4]{1,2,0:T(4,128)}), s32[64,8,4]{1,2,0:T(4,128)S(1)}, u32[]{:S(2)}, u32[]{:S(2)}) async-start(s32[64,8,4]{1,2,0:T(4,128)} %broadcast_in_dim.46), calls=%async_computation.2 | async-start | bytes 262144 | tf_op jit(solution)/shard_map/all_to_all | solution.py:121
  127.6 26.6 %all-to-all-start.3 = ((f32[64,1,128]{2,1,0:T(1,128)}), f32[64,1,128]{2,1,0:T(1,128)S(1)}, u32[]{:S(2)}, u32[]{:S(2)}) async-start(f32[64,1,128]{2,1,0:T(1,128)} %reshape.236), calls=%async_computation.3 | async-start | bytes 65536 | tf_op jit(solution)/shard_map/all_to_all | solution.py:129
  157.8 11.1 %all-to-all-start.4 = ((f32[8,2,4]{2,1,0:T(2,128)}), f32[8,2,4]{2,1,0:T(2,128)S(1)}, u32[]{:S(2)}, u32[]{:S(2)}) async-start(f32[8,2,4]{2,1,0:T(2,128)} %gather_fusion.5), calls=%async_computation.4 | async-start | bytes 16384 | tf_op jit(solution)/shard_map/all_to_all | solution.py:142
Sparse Core Ops, SparseCore 0:
  20.5 93.6 all-gather.1

commit v9 on v8

--- a/solution.py
+++ b/solution.py
@@ -9,7 +9,7 @@
 
 VREAL = 49155
 INTERPRET = False
-ROW_BLOCK = 512
+ROW_BLOCK = 1024
 
 
 def stats_kernel(offset_ref, emb_ref, rows_ref, marks_ref, out_ref):

time: 178 us -> 178 us (level)
  no operation moved by 1% of the time
where the time goes in v9:
time: 178 us; the launch traced here: 177 us
  waiting for transfers between devices  74.2 us (42%)
  starting transfers between devices  43.5 us (24%)
  local copies, waits for them, and re-layouts  15.2 us (9%)
  between operations  14.2 us (8%)
  blocking collectives  11 us (6%)
  Pallas kernels  10.6 us (6%)
  other arithmetic  8.82 us (5%)
    all_gather x1, waiting for transfers between devices, gather_rows(): rows = lax.all_gather(rows, name, axis=1, tiled=True)  40.2 us
    all_to_all x1, waiting for transfers between devices, local(): lax.all_to_all(spread, tensor_axes, split_axis=0, concat_axis=0, tiled=True)  16.1 us
    all_to_all x1, starting transfers between devices, local(): lax.all_to_all(spread, tensor_axes, split_axis=0, concat_axis=0, tiled=True)  14.1 us
    all_to_all x1, waiting for transfers between devices, local(): lax.all_to_all(stats, tensor_axes, split_axis=0, concat_axis=0, tiled=True)  13.3 us
    all_to_all x1, starting transfers between devices, local(): lax.all_to_all(stats, tensor_axes, split_axis=0, concat_axis=0, tiled=True)  13.2 us
    all_to_all x1, blocking collectives, gather_rows(): got = lax.all_to_all(spread, name, split_axis=0, concat_axis=0, tiled=True)  11 us
    pallas_call x1, Pallas kernels, row_stats(): pl.pallas_call(stats_kernel, grid=(n // block,), in_specs=[pl.BlockSpec(m...  10.6 us
    all_to_all x1, starting transfers between devices, local(): lax.all_to_all(marked[send_order], 'dp', split_axis=0, concat_axis=0, til...  9.55 us
  transfers between devices with their start and end apart: 5, of which 4 were waited for; matrix products, arithmetic and copies ran while one was open for 8% of the time, Pallas kernels for 0%

profile of v9, /device:TPU:1, one launch (start us, length us, event | category | flops | bytes accessed | tf_op | source)
XLA Modules:
  0.0 177.5 jit_solution(2489367336947438808)
XLA Ops:
  7.2 1.0 fusion
  8.3 1.0 fusion.2
  9.3 11.0 %all_to_all.32 = bf16[4,8,4,1536]{3,1,2,0:T(8,128)(2,1)} all-to-all(bf16[4,8,4,1536]{3,1,2,0:T(8,128)(2,1)S(1)} %broadcast_in_dim.45), channel_id=1, replica_groups=mesh['dp'=8,'tx'=4,'tz'=16] {'tx'}, dimensions={0} | all-to-all | bytes 786432 | tf_op jit(solution)/shard_map/all_to_all | solution.py:78
  20.3 0.8 copy.34
  22.5 1.3 gather_fusion.1
  23.9 1.0 sort.65
  24.9 1.1 gather_fusion.2
  26.0 9.5 %all-to-all-start = ((s32[8,1,4]{2,1,0:T(1,128)}), s32[8,1,4]{2,1,0:T(1,128)S(1)}, u32[]{:S(2)}, u32[]{:S(2)}) async-start(s32[8,1,4]{2,1,0:T(1,128)} %bitcast.22), calls=%async_computation | async-start | bytes 8192 | tf_op jit(solution)/shard_map/all_to_all | solution.py:118
  36.3 2.0 %sort.66 = (s32[64]{0:T(128)}, s32[64]{0:T(128)S(1)}) sort(s32[64]{0:T(128)S(1)} %compare_convert_fusion, s32[64]{0:T(128)S(1)} %iota.27), dimensions={0}, to_apply=%region_1.2 | sort | flops 384 | bytes 1024 | tf_op jit(solution)/shard_map/jit(argsort)/sort | solution.py:108
  38.3 1.3 gather_fusion.3
  39.6 1.0 sort.67
  41.9 14.1 %all-to-all-start.2 = ((s32[64,8,4]{1,2,0:T(4,128)}), s32[64,8,4]{1,2,0:T(4,128)S(1)}, u32[]{:S(2)}, u32[]{:S(2)}) async-start(s32[64,8,4]{1,2,0:T(4,128)} %broadcast_in_dim.46), calls=%async_computation.2 | async-start | bytes 262144 | tf_op jit(solution)/shard_map/all_to_all | solution.py:121
  56.1 1.0 sort.68
  57.1 16.1 %all-to-all-done.2 = s32[64,8,4]{1,2,0:T(4,128)S(1)} async-done(((s32[64,8,4]{1,2,0:T(4,128)}), s32[64,8,4]{1,2,0:T(4,128)S(1)}, u32[]{:S(2)}, u32[]{:S(2)}) %all-to-all-start.2) | async-done | bytes 8224 | tf_op jit(solution)/shard_map/all_to_all | solution.py:121
  73.2 0.8 reshape_reshape.3.marks_ref
  73.9 40.2 %all-gather.2.cloned.1.call-done = bf16[8,256,1536]{2,0,1:T(8,128)(2,1)} async-done(((bf16[8,16,1536]{2,0,1:T(8,128)(2,1)}), bf16[8,256,1536]{2,0,1:T(8,128)(2,1)}) %all-gather.2.cloned.1.call-update) | async-done | bytes 6291472 | tf_op jit(solution)/shard_map/all_gather | solution.py:81
  114.1 10.6 %shard_map.86 = f32[4,2048]{1,0:T(4,128)} custom-call(s32[1]{0:T(128)} %bitcast.3.offset_ref, bf16[776,1536]{1,0:T(8,128)(2,1)} %emb_ref.1, bf16[2048,1536]{1,0:T(8,128)(2,1)} %bitcast.70, s32[1,2048]{1,0:T(1,128)} %reshape_reshape.3.marks_ref), custom_call_target="tpu_custom_call" | custom-call | flops 4882169856 | bytes 8716288 | tf_op jit(solution)/shard_map/pallas_call | solution.py:35
  124.7 1.4 reshape.174
  126.2 1.1 reshape.236
  127.4 13.2 %all-to-all-start.3 = ((f32[64,1,128]{2,1,0:T(1,128)}), f32[64,1,128]{2,1,0:T(1,128)S(1)}, u32[]{:S(2)}, u32[]{:S(2)}) async-start(f32[64,1,128]{2,1,0:T(1,128)} %reshape.236), calls=%async_computation.3 | async-start | bytes 65536 | tf_op jit(solution)/shard_map/all_to_all | solution.py:129
  140.6 13.3 %all-to-all-done.3 = f32[64,1,128]{2,1,0:T(1,128)S(1)} async-done(((f32[64,1,128]{2,1,0:T(1,128)}), f32[64,1,128]{2,1,0:T(1,128)S(1)}, u32[]{:S(2)}, u32[]{:S(2)}) %all-to-all-start.3) | async-done | bytes 32800 | tf_op jit(solution)/shard_map/all_to_all | solution.py:129
  156.4 1.2 gather_fusion.5
  157.6 6.5 %all-to-all-start.4 = ((f32[8,2,4]{2,1,0:T(2,128)}), f32[8,2,4]{2,1,0:T(2,128)S(1)}, u32[]{:S(2)}, u32[]{:S(2)}) async-start(f32[8,2,4]{2,1,0:T(2,128)} %gather_fusion.5), calls=%async_computation.4 | async-start | bytes 16384 | tf_op jit(solution)/shard_map/all_to_all | solution.py:142
  164.1 4.6 %all-to-all-done.4 = f32[8,2,4]{2,1,0:T(2,128)S(1)} async-done(((f32[8,2,4]{2,1,0:T(2,128)}), f32[8,2,4]{2,1,0:T(2,128)S(1)}, u32[]{:S(2)}, u32[]{:S(2)}) %all-to-all-start.4) | async-done | bytes 288 | tf_op jit(solution)/shard_map/all_to_all | solution.py:142
  (53 shorter events, 8.2 us)
Async XLA Ops:
  7.2 14.7 %copy-start = (s32[64]{0:T(128)S(1)}, s32[64]{0:T(128)}, u32[]{:S(2)}) copy-start(s32[64]{0:T(128)} %param.11) | copy-start | bytes 772
  7.2 106.9 %all-gather.2.cloned.1.call-start = ((), (), s32[]{:S(2)}) async-start(), calls=%async_computation.5 | async-start | bytes 6684672 | tf_op jit(solution)/shard_map/all_gather | solution.py:81
  26.0 14.6 %all-to-all-start = ((s32[8,1,4]{2,1,0:T(1,128)}), s32[8,1,4]{2,1,0:T(1,128)S(1)}, u32[]{:S(2)}, u32[]{:S(2)}) async-start(s32[8,1,4]{2,1,0:T(1,128)} %bitcast.22), calls=%async_computation | async-start | bytes 8192 | tf_op jit(solution)/shard_map/all_to_all | solution.py:118
  41.9 31.2 %all-to-all-start.2 = ((s32[64,8,4]{1,2,0:T(4,128)}), s32[64,8,4]{1,2,0:T(4,128)S(1)}, u32[]{:S(2)}, u32[]{:S(2)}) async-start(s32[64,8,4]{1,2,0:T(4,128)} %broadcast_in_dim.46), calls=%async_computation.2 | async-start | bytes 262144 | tf_op jit(solution)/shard_map/all_to_all | solution.py:121
  127.4 26.6 %all-to-all-start.3 = ((f32[64,1,128]{2,1,0:T(1,128)}), f32[64,1,128]{2,1,0:T(1,128)S(1)}, u32[]{:S(2)}, u32[]{:S(2)}) async-start(f32[64,1,128]{2,1,0:T(1,128)} %reshape.236), calls=%async_computation.3 | async-start | bytes 65536 | tf_op jit(solution)/shard_map/all_to_all | solution.py:129
  157.6 11.1 %all-to-all-start.4 = ((f32[8,2,4]{2,1,0:T(2,128)}), f32[8,2,4]{2,1,0:T(2,128)S(1)}, u32[]{:S(2)}, u32[]{:S(2)}) async-start(f32[8,2,4]{2,1,0:T(2,128)} %gather_fusion.5), calls=%async_computation.4 | async-start | bytes 16384 | tf_op jit(solution)/shard_map/all_to_all | solution.py:142
Sparse Core Ops, SparseCore 0:
  20.5 93.6 all-gather.1

commit v10 on v9

--- a/solution.py
+++ b/solution.py
@@ -9,7 +9,7 @@
 
 VREAL = 49155
 INTERPRET = False
-ROW_BLOCK = 1024
+ROW_BLOCK = 256
 
 
 def stats_kernel(offset_ref, emb_ref, rows_ref, marks_ref, out_ref):

time: 178 us -> 179 us (level)
  no operation moved by 1% of the time
where the time goes in v10:
time: 179 us; the launch traced here: 178 us
  waiting for transfers between devices  74.2 us (41%)
  starting transfers between devices  43.5 us (24%)
  local copies, waits for them, and re-layouts  15.2 us (8%)
  between operations  14.2 us (8%)
  Pallas kernels  11.3 us (6%)
  blocking collectives  11 us (6%)
  other arithmetic  8.82 us (5%)
    all_gather x1, waiting for transfers between devices, gather_rows(): rows = lax.all_gather(rows, name, axis=1, tiled=True)  40.2 us
    all_to_all x1, waiting for transfers between devices, local(): lax.all_to_all(spread, tensor_axes, split_axis=0, concat_axis=0, tiled=True)  16.1 us
    all_to_all x1, starting transfers between devices, local(): lax.all_to_all(spread, tensor_axes, split_axis=0, concat_axis=0, tiled=True)  14.1 us
    all_to_all x1, waiting for transfers between devices, local(): lax.all_to_all(stats, tensor_axes, split_axis=0, concat_axis=0, tiled=True)  13.3 us
    all_to_all x1, starting transfers between devices, local(): lax.all_to_all(stats, tensor_axes, split_axis=0, concat_axis=0, tiled=True)  13.2 us
    pallas_call x1, Pallas kernels, row_stats(): pl.pallas_call(stats_kernel, grid=(n // block,), in_specs=[pl.BlockSpec(m...  11.3 us
    all_to_all x1, blocking collectives, gather_rows(): got = lax.all_to_all(spread, name, split_axis=0, concat_axis=0, tiled=True)  11 us
    all_to_all x1, starting transfers between devices, local(): lax.all_to_all(marked[send_order], 'dp', split_axis=0, concat_axis=0, til...  9.55 us
  transfers between devices with their start and end apart: 5, of which 4 were waited for; matrix products, arithmetic and copies ran while one was open for 8% of the time, Pallas kernels for 0%

profile of v10, /device:TPU:1, one launch (start us, length us, event | category | flops | bytes accessed | tf_op | source)
XLA Modules:
  0.0 178.2 jit_solution(16711436320740064095)
XLA Ops:
  7.2 1.0 fusion
  8.3 1.0 fusion.2
  9.3 11.0 %all_to_all.32 = bf16[4,8,4,1536]{3,1,2,0:T(8,128)(2,1)} all-to-all(bf16[4,8,4,1536]{3,1,2,0:T(8,128)(2,1)S(1)} %broadcast_in_dim.45), channel_id=1, replica_groups=mesh['dp'=8,'tx'=4,'tz'=16] {'tx'}, dimensions={0} | all-to-all | bytes 786432 | tf_op jit(solution)/shard_map/all_to_all | solution.py:78
  20.3 0.8 copy.34
  22.5 1.3 gather_fusion.1
  23.9 1.0 sort.65
  24.9 1.1 gather_fusion.2
  26.0 9.5 %all-to-all-start = ((s32[8,1,4]{2,1,0:T(1,128)}), s32[8,1,4]{2,1,0:T(1,128)S(1)}, u32[]{:S(2)}, u32[]{:S(2)}) async-start(s32[8,1,4]{2,1,0:T(1,128)} %bitcast.22), calls=%async_computation | async-start | bytes 8192 | tf_op jit(solution)/shard_map/all_to_all | solution.py:118
  36.3 2.0 %sort.66 = (s32[64]{0:T(128)}, s32[64]{0:T(128)S(1)}) sort(s32[64]{0:T(128)S(1)} %compare_convert_fusion, s32[64]{0:T(128)S(1)} %iota.27), dimensions={0}, to_apply=%region_1.2 | sort | flops 384 | bytes 1024 | tf_op jit(solution)/shard_map/jit(argsort)/sort | solution.py:108
  38.3 1.3 gather_fusion.3
  39.6 1.0 sort.67
  41.9 14.1 %all-to-all-start.2 = ((s32[64,8,4]{1,2,0:T(4,128)}), s32[64,8,4]{1,2,0:T(4,128)S(1)}, u32[]{:S(2)}, u32[]{:S(2)}) async-start(s32[64,8,4]{1,2,0:T(4,128)} %broadcast_in_dim.46), calls=%async_computation.2 | async-start | bytes 262144 | tf_op jit(solution)/shard_map/all_to_all | solution.py:121
  56.1 1.0 sort.68
  57.1 16.1 %all-to-all-done.2 = s32[64,8,4]{1,2,0:T(4,128)S(1)} async-done(((s32[64,8,4]{1,2,0:T(4,128)}), s32[64,8,4]{1,2,0:T(4,128)S(1)}, u32[]{:S(2)}, u32[]{:S(2)}) %all-to-all-start.2) | async-done | bytes 8224 | tf_op jit(solution)/shard_map/all_to_all | solution.py:121
  73.2 0.8 reshape_reshape.3.marks_ref
  73.9 40.2 %all-gather.2.cloned.1.call-done = bf16[8,256,1536]{2,0,1:T(8,128)(2,1)} async-done(((bf16[8,16,1536]{2,0,1:T(8,128)(2,1)}), bf16[8,256,1536]{2,0,1:T(8,128)(2,1)}) %all-gather.2.cloned.1.call-update) | async-done | bytes 6291472 | tf_op jit(solution)/shard_map/all_gather | solution.py:81
  114.1 11.3 %shard_map.86 = f32[4,2048]{1,0:T(4,128)} custom-call(s32[1]{0:T(128)} %bitcast.3.offset_ref, bf16[776,1536]{1,0:T(8,128)(2,1)} %emb_ref.1, bf16[2048,1536]{1,0:T(8,128)(2,1)} %bitcast.70, s32[1,2048]{1,0:T(1,128)} %reshape_reshape.3.marks_ref), custom_call_target="tpu_custom_call" | custom-call | flops 4882169856 | bytes 8716288 | tf_op jit(solution)/shard_map/pallas_call | solution.py:35
  125.4 1.4 reshape.174
  126.9 1.1 reshape.236
  128.1 13.2 %all-to-all-start.3 = ((f32[64,1,128]{2,1,0:T(1,128)}), f32[64,1,128]{2,1,0:T(1,128)S(1)}, u32[]{:S(2)}, u32[]{:S(2)}) async-start(f32[64,1,128]{2,1,0:T(1,128)} %reshape.236), calls=%async_computation.3 | async-start | bytes 65536 | tf_op jit(solution)/shard_map/all_to_all | solution.py:129
  141.3 13.3 %all-to-all-done.3 = f32[64,1,128]{2,1,0:T(1,128)S(1)} async-done(((f32[64,1,128]{2,1,0:T(1,128)}), f32[64,1,128]{2,1,0:T(1,128)S(1)}, u32[]{:S(2)}, u32[]{:S(2)}) %all-to-all-start.3) | async-done | bytes 32800 | tf_op jit(solution)/shard_map/all_to_all | solution.py:129
  157.1 1.2 gather_fusion.5
  158.3 6.5 %all-to-all-start.4 = ((f32[8,2,4]{2,1,0:T(2,128)}), f32[8,2,4]{2,1,0:T(2,128)S(1)}, u32[]{:S(2)}, u32[]{:S(2)}) async-start(f32[8,2,4]{2,1,0:T(2,128)} %gather_fusion.5), calls=%async_computation.4 | async-start | bytes 16384 | tf_op jit(solution)/shard_map/all_to_all | solution.py:142
  164.8 4.6 %all-to-all-done.4 = f32[8,2,4]{2,1,0:T(2,128)S(1)} async-done(((f32[8,2,4]{2,1,0:T(2,128)}), f32[8,2,4]{2,1,0:T(2,128)S(1)}, u32[]{:S(2)}, u32[]{:S(2)}) %all-to-all-start.4) | async-done | bytes 288 | tf_op jit(solution)/shard_map/all_to_all | solution.py:142
  (53 shorter events, 8.2 us)
Async XLA Ops:
  7.2 14.7 %copy-start = (s32[64]{0:T(128)S(1)}, s32[64]{0:T(128)}, u32[]{:S(2)}) copy-start(s32[64]{0:T(128)} %param.11) | copy-start | bytes 772
  7.2 106.9 %all-gather.2.cloned.1.call-start = ((), (), s32[]{:S(2)}) async-start(), calls=%async_computation.5 | async-start | bytes 6684672 | tf_op jit(solution)/shard_map/all_gather | solution.py:81
  26.0 14.6 %all-to-all-start = ((s32[8,1,4]{2,1,0:T(1,128)}), s32[8,1,4]{2,1,0:T(1,128)S(1)}, u32[]{:S(2)}, u32[]{:S(2)}) async-start(s32[8,1,4]{2,1,0:T(1,128)} %bitcast.22), calls=%async_computation | async-start | bytes 8192 | tf_op jit(solution)/shard_map/all_to_all | solution.py:118
  41.9 31.2 %all-to-all-start.2 = ((s32[64,8,4]{1,2,0:T(4,128)}), s32[64,8,4]{1,2,0:T(4,128)S(1)}, u32[]{:S(2)}, u32[]{:S(2)}) async-start(s32[64,8,4]{1,2,0:T(4,128)} %broadcast_in_dim.46), calls=%async_computation.2 | async-start | bytes 262144 | tf_op jit(solution)/shard_map/all_to_all | solution.py:121
  128.1 26.6 %all-to-all-start.3 = ((f32[64,1,128]{2,1,0:T(1,128)}), f32[64,1,128]{2,1,0:T(1,128)S(1)}, u32[]{:S(2)}, u32[]{:S(2)}) async-start(f32[64,1,128]{2,1,0:T(1,128)} %reshape.236), calls=%async_computation.3 | async-start | bytes 65536 | tf_op jit(solution)/shard_map/all_to_all | solution.py:129
  158.3 11.1 %all-to-all-start.4 = ((f32[8,2,4]{2,1,0:T(2,128)}), f32[8,2,4]{2,1,0:T(2,128)S(1)}, u32[]{:S(2)}, u32[]{:S(2)}) async-start(f32[8,2,4]{2,1,0:T(2,128)} %gather_fusion.5), calls=%async_computation.4 | async-start | bytes 16384 | tf_op jit(solution)/shard_map/all_to_all | solution.py:142
Sparse Core Ops, SparseCore 0:
  20.5 93.6 all-gather.1
